TPU v7x, 32 devices: a whole 2x2x4 slice. The times are simulated.
32 devices in a mesh: grp: 2 (over x), dec: 16 (over z, y, core).
Axes of the slice: x: 2, y: 2, z: 4, core: 2. Of those that a mesh axis runs over, the one named last changes fastest.
Arguments:
- latents: bfloat16 [4096, 4, 512], P(('grp', 'dec')), parts along dimension 0, may hold values from -6 to 6
- cache: bfloat16 [4096, 7, 512], P(('grp', 'dec')), parts along dimension 0, may hold values from -6 to 6
- panel_slot: int32 [4096], P(('grp', 'dec')), parts along dimension 0, may hold values from 0 to 2047, as said below
- cache_slot: int32 [4096], P(('grp', 'dec')), parts along dimension 0, may hold values from 0 to 2047, as said below
- frames_valid: int32 [4096], P(('grp', 'dec')), parts along dimension 0, may hold values from 1 to 4
- up_weight: float32 [4, 512], replicated, may hold values from -3 to 3
- conv_weight: bfloat16 [7, 512, 1024], replicated, may hold values from -0.09375 to 0.09375
- conv_bias: float32 [1024], replicated, may hold values from -0.5 to 0.5
Outputs:
- decoded: bfloat16 [4096, 8, 1024], P(('grp', 'dec')), parts along dimension 0
- new_cache: bfloat16 [4096, 7, 512], P(('grp', 'dec')), parts along dimension 0
There are 2 independent parts, one for each index of `grp`. A program takes and returns all parts, laid end to end along the dimension named above; an argument that names none is the same for every part. Nothing has to cross between parts.
Inputs may be any that keep to these rules, and one draw needn't show every extreme that they name: `panel_slot`: A permutation of the owner slots. Each device's rows go to owner devices in the same counts; at most 9 rows of one device go to one owner device, and every device has one owner device that receives exactly 9 of its rows. `cache_slot`: A permutation of the owner slots. Exactly 64 of each device's slots go to other devices, the rest keep their slot; at most 5 go from one device to one other device, and every device sends exactly 5 to one of them.
All inputs are finite; a program needn't handle non-finite values.
Results may differ from a plain program's by a relative error of at most 0.0034.
Values may be sent and summed in bfloat16 or wider, within the bound.
No kernel may reach another device: no remote copies, remote signals or barrier semaphores. Data moves between devices by JAX's collectives and lax.ppermute only.
A program may use at most 64 MiB of HBM per device.

v0:
```python
import jax
import jax.numpy as jnp
from jax import lax
from jax.sharding import PartitionSpec as P


def buckets(rows, target, local, capacity, number):
    hits = (target[:, None] == jnp.arange(number, dtype=jnp.int32)[None, :]).astype(jnp.int32)
    rank = jnp.sum(hits * (jnp.cumsum(hits, axis=0) - 1), axis=1)
    place = jnp.where(target >= 0, target * capacity + rank, -1)
    picker = (place[:, None] == jnp.arange(number * capacity, dtype=jnp.int32)[None, :]).astype(
        jnp.bfloat16
    )
    packed = jnp.dot(picker.T, rows, preferred_element_type=jnp.float32).astype(jnp.bfloat16)
    labels = (
        jnp.sum(picker.T.astype(jnp.float32) * (local + 1).astype(jnp.float32)[None, :], axis=1)
        - 1.0
    )
    width = rows.shape[1]
    return (
        packed.reshape(number, capacity, width),
        labels.reshape(number, capacity).astype(jnp.bfloat16),
    )


def settle(received, labels, streams):
    width = received.shape[-1]
    flat_rows = received.reshape(-1, width)
    flat_labels = labels.reshape(-1).astype(jnp.float32)
    picker = (flat_labels[:, None] == jnp.arange(streams, dtype=jnp.float32)[None, :]).astype(
        jnp.bfloat16
    )
    return jnp.dot(picker.T, flat_rows, preferred_element_type=jnp.float32)


def body(latents, cache, panel_slot, cache_slot, frames_valid, up_weight, conv_weight, conv_bias):
    number = lax.axis_size("dec")
    myself = lax.axis_index("dec")
    streams = latents.shape[0]
    frames = latents.shape[1]
    channels = latents.shape[2]
    rows_kept = cache.shape[1]
    outward = conv_weight.shape[2]
    taps = conv_weight.shape[0]
    pair_cap = max(2, (streams + number - 2) // (number - 1))
    mig_cap = max(2, (streams // 2 + number - 3) // (number - 2))
    panel_width = frames * channels
    cache_width = rows_kept * channels
    flat_latents = latents.reshape(streams, panel_width)
    flat_cache = cache.reshape(streams, cache_width)
    panel_owner = panel_slot // streams
    panel_local = panel_slot % streams
    cache_owner = cache_slot // streams
    cache_local = cache_slot % streams
    moving = cache_owner != myself
    staying = jnp.logical_not(moving)
    stay_pick = (
        staying[:, None] & (cache_local[:, None] == jnp.arange(streams, dtype=jnp.int32)[None, :])
    ).astype(jnp.bfloat16)
    kept = jnp.dot(stay_pick.T, flat_cache, preferred_element_type=jnp.float32)
    cache_send, cache_labels = buckets(
        flat_cache, jnp.where(moving, cache_owner, -1), cache_local, mig_cap, number
    )
    panel_send, panel_labels = buckets(flat_latents, panel_owner, panel_local, pair_cap, number)
    joint = jnp.concatenate(
        [panel_send.reshape(number, -1), cache_send.reshape(number, -1)], axis=1
    )
    joint_labels = jnp.concatenate([panel_labels, cache_labels], axis=1)
    joint_recv, joint_recv_labels = (
        lax.all_to_all(joint, "dec", split_axis=0, concat_axis=0, tiled=True),
        lax.all_to_all(joint_labels, "dec", split_axis=0, concat_axis=0, tiled=True),
    )
    split_at = pair_cap * panel_width
    panel_recv = joint_recv[:, :split_at].reshape(number, pair_cap, panel_width)
    cache_recv = joint_recv[:, split_at:].reshape(number, mig_cap, cache_width)
    panels = settle(panel_recv, joint_recv_labels[:, :pair_cap], streams)
    arrived = settle(cache_recv, joint_recv_labels[:, pair_cap:], streams)
    latent_rows = panels.astype(jnp.bfloat16).reshape(streams, frames, channels)
    owned = (kept + arrived).astype(jnp.bfloat16).reshape(streams, rows_kept, channels)
    previous = jnp.concatenate([owned[:, 0:1], latent_rows], axis=1)
    current = previous[:, 1:].astype(jnp.float32)
    earlier = previous[:, :-1].astype(jnp.float32)
    even = up_weight[0] * current + up_weight[2] * earlier
    odd = up_weight[1] * current + up_weight[3] * earlier
    upsampled = (
        jnp.stack([even, odd], axis=2).reshape(streams, 2 * frames, channels).astype(jnp.bfloat16)
    )
    extended = jnp.concatenate([owned[:, 1:], upsampled], axis=1)
    total = jnp.zeros((streams * 2 * frames, outward), jnp.float32) + conv_bias
    for tap in range(taps):
        window = extended[:, tap : tap + 2 * frames].reshape(streams * 2 * frames, channels)
        total = total + jnp.dot(window, conv_weight[tap], preferred_element_type=jnp.float32)
    active = jax.nn.elu(total).reshape(streams, 2 * frames, outward)
    position = jnp.arange(2 * frames, dtype=jnp.int32)
    keep = position[None, :] < 2 * frames_valid[:, None]
    decoded = jnp.where(keep[:, :, None], active, 0.0).astype(jnp.bfloat16)
    pick_latent = (
        jnp.arange(frames + 1, dtype=jnp.int32)[None, :] == frames_valid[:, None]
    ).astype(jnp.bfloat16)
    last_latent = jnp.einsum(
        "sf,sfc->sc", pick_latent, previous, preferred_element_type=jnp.float32
    )
    target = 2 * frames_valid[:, None, None] + jnp.arange(taps - 1, dtype=jnp.int32)[None, :, None]
    pick_rows = (
        jnp.arange(taps - 1 + 2 * frames, dtype=jnp.int32)[None, None, :] == target
    ).astype(jnp.bfloat16)
    last_rows = jnp.einsum("sjt,stc->sjc", pick_rows, extended, preferred_element_type=jnp.float32)
    new_cache = jnp.concatenate([last_latent[:, None], last_rows], axis=1).astype(jnp.bfloat16)
    return (decoded, new_cache)


def solution(mesh):
    in_specs = (
        P(("grp", "dec"), None, None),
        P(("grp", "dec"), None, None),
        P(("grp", "dec")),
        P(("grp", "dec")),
        P(("grp", "dec")),
        P(),
        P(),
        P(),
    )
    out_specs = (P(("grp", "dec"), None, None), P(("grp", "dec"), None, None))
    return jax.shard_map(body, mesh=mesh, in_specs=in_specs, out_specs=out_specs, check_vma=False)
```

profile of v0, /device:TPU:13, one launch (start us, length us, event | category | flops | bytes accessed | tf_op | source)
XLA Modules:
  0.0 95.0 jit_solution(4575831757905589145)
XLA Ops:
  0.6 0.7 fusion.73
  1.4 0.7 compare_not_fusion
  2.2 0.2 reduce_window_sum.18
  2.5 0.7 add_convert_fusion.2
  3.5 0.2 reduce_window_sum.17
  3.7 0.2 select_reduce_fusion.1
  4.2 0.6 copy.36
  4.8 6.6 %all-to-all-start = ((bf16[16,1,14]{2,1,0:T(2,128)(2,1)}), bf16[16,1,14]{2,1,0:T(2,128)(2,1)S(1)}, u32[]{:S(2)}, u32[]{:S(2)}) async-start(bf16[16,1,14]{2,1,0:T(2,128)(2,1)} %copy.36), calls=%async_computation | async-start | bytes 16384 | tf_op jit(solution)/shard_map/all_to_all | solution.py:71
  11.3 1.1 %copy.49 = bf16[16,8,4,512]{3,1,2,0:T(8,128)(2,1)S(1)} copy(bf16[16,8,4,512]{3,2,1,0:T(4,128)(2,1)} %bitcast.88) | data formatting | bytes 1048576
  12.5 0.4 convolution_convert_fusion.1
  12.9 0.9 reshape_reshape.12
  13.8 0.6 copy.35
  14.4 0.5 convolution_convert_fusion
  15.0 0.6 reshape_reshape.13
  15.6 0.5 broadcast.142
  16.1 1.5 %reduce = bf16[16,36352]{1,0:T(8,128)(2,1)S(1)} reduce(bf16[16,1,36352]{2,0,1:T(8,128)(2,1)S(1)} %maximum_bitcast_fusion, bf16[]{:T(256)} %broadcast.142), dimensions={1}, to_apply=%copy.37.reduce_sub_computation | reduce | bytes 2326530 | tf_op jit(solution)/shard_map/all_to_all | solution.py:70
  17.7 1.2 %reshape.155 = bf16[16,2,18176]{2,1,0:T(2,128)(2,1)} reshape(bf16[16,36352]{1,0:T(8,128)(2,1)S(1)} %reduce) | data formatting | bytes 2326528
  18.9 6.0 %all-to-all-start.1 = ((bf16[16,2,18176]{2,1,0:T(2,128)(2,1)}), bf16[16,2,18176]{2,1,0:T(2,128)(2,1)}, u32[]{:S(2)}, u32[]{:S(2)}) async-start(bf16[16,2,18176]{2,1,0:T(2,128)(2,1)} %reshape.155), calls=%async_computation.1 | async-start | bytes 2326528 | tf_op jit(solution)/shard_map/all_to_all | solution.py:70
  25.1 0.7 iota_add_fusion
  26.1 26.3 %all-to-all-done.1 = bf16[16,2,18176]{2,1,0:T(2,128)(2,1)} async-done(((bf16[16,2,18176]{2,1,0:T(2,128)(2,1)}), bf16[16,2,18176]{2,1,0:T(2,128)(2,1)}, u32[]{:S(2)}, u32[]{:S(2)}) %all-to-all-start.1) | async-done | bytes 1163296 | tf_op jit(solution)/shard_map/all_to_all | solution.py:70
  52.4 4.3 %reshape.156 = bf16[16,1,36352]{2,1,0:T(2,128)(2,1)S(1)} reshape(bf16[16,2,18176]{2,1,0:T(2,128)(2,1)} %all-to-all-done.1) | data formatting | bytes 2326528
  56.9 0.6 reshape_reshape.14
  57.5 0.5 fusion.64
  58.0 0.5 fusion
  58.5 0.6 copy.38
  59.2 0.9 reshape_reshape.15
  60.1 0.4 convolution_convert_fusion.2
  60.5 0.4 reshape.143
  60.9 0.2 copy.40
  61.1 1.0 %fusion.8 = (bf16[128,4,1,512]{3,1,0,2:T(4,128)(2,1)S(1)}, bf16[128,4,512]{2,1,0:T(4,128)(2,1)S(1)}) fusion(bf16[128,4,512]{2,1,0:T(4,128)(2,1)S(1)} %reshape.143, bf16[128,1,512]{2,1,0:T(2,128)(2,1)S(1)} %copy.40, f32[512]{0:T(512)S(1)} %bitcast.94, f32[512]{0:T(512)S(1)} %bitcast.93, f32[512]{0:T(512)S(1)} %bitcast.95, f32[512]{0:T(512)S(1)} %bitcast.96), kind=kLoop, calls=%fused_computation.34 | loop fusion | flops 3407872 | bytes 1712128 | tf_op jit(solution)/shard_map/stack | solution.py:86
  62.2 0.8 copy.41
  63.0 0.7 stack.10
  63.8 2.4 %maximum_convert_fusion = bf16[128,4,2,512]{3,2,1,0:T(2,128)(2,1)S(1)} fusion(bf16[128,4,1,512]{3,2,1,0:T(2,128)(2,1)S(1)} %stack.10, bf16[128,4,1,512]{3,2,1,0:T(2,128)(2,1)S(1)} %copy.41), kind=kLoop, calls=%fused_computation.25 | loop fusion | flops 2097152 | bytes 2097152 | tf_op jit(solution)/shard_map/convert_element_type | solution.py:86
  66.2 0.4 convert_element_type.124
  66.7 1.3 %convert_element_type.125 = bf16[1024,512]{1,0:T(8,128)(2,1)} reshape(bf16[128,4,2,512]{3,2,1,0:T(2,128)(2,1)S(1)} %maximum_convert_fusion) | data formatting | bytes 2097152 | tf_op jit(solution)/shard_map/convert_element_type | solution.py:86
  68.0 1.1 %copy.48 = bf16[128,6,512]{2,1,0:T(8,128)(2,1)S(1)} copy(bf16[128,6,512]{0,2,1:T(8,128)(2,1)S(1)} %slice.98) | data formatting | bytes 1572864
  69.1 2.9 %fusion.12 = f32[1024,1024]{1,0:T(8,128)S(1)} fusion(bf16[128,6,512]{2,1,0:T(8,128)(2,1)S(1)} %copy.48, bf16[128,8,512]{2,1,0:T(8,128)(2,1)S(1)} %convert_element_type.124, bf16[7,512,1024]{2,1,0:T(8,128)(2,1)} %param.14), kind=kOutput, calls=%fused_computation.38 | convolution fusion | flops 1075838976 | bytes 7077888 | tf_op jit(solution)/shard_map/dot_general | solution.py:92
  72.0 2.7 %fusion.16 = f32[1024,1024]{1,0:T(8,128)S(1)} fusion(bf16[128,6,512]{2,1,0:T(8,128)(2,1)S(1)} %copy.48, bf16[128,8,512]{2,1,0:T(8,128)(2,1)S(1)} %convert_element_type.124, bf16[7,512,1024]{2,1,0:T(8,128)(2,1)} %param.14), kind=kOutput, calls=%fused_computation.41 | convolution fusion | flops 1075838976 | bytes 7077888 | tf_op jit(solution)/shard_map/dot_general | solution.py:92
  74.7 1.3 %fusion.20 = f32[1024,1024]{1,0:T(8,128)S(1)} fusion(bf16[128,6,512]{2,1,0:T(8,128)(2,1)S(1)} %copy.48, bf16[128,8,512]{2,1,0:T(8,128)(2,1)S(1)} %convert_element_type.124, bf16[7,512,1024]{2,1,0:T(8,128)(2,1)S(1)} %bitcast.90), kind=kOutput, calls=%fused_computation.44 | convolution fusion | flops 1075838976 | bytes 7340032 | tf_op jit(solution)/shard_map/dot_general | solution.py:92
  76.1 1.3 %fusion.24 = f32[1024,1024]{1,0:T(8,128)S(1)} fusion(bf16[128,6,512]{2,1,0:T(8,128)(2,1)S(1)} %copy.48, bf16[128,8,512]{2,1,0:T(8,128)(2,1)S(1)} %convert_element_type.124, bf16[7,512,1024]{2,1,0:T(8,128)(2,1)S(1)} %bitcast.90), kind=kOutput, calls=%fused_computation.47 | convolution fusion | flops 1075838976 | bytes 7340032 | tf_op jit(solution)/shard_map/dot_general | solution.py:92
  77.4 3.0 %fusion.28 = f32[1024,1024]{1,0:T(8,128)S(1)} fusion(bf16[128,6,512]{2,1,0:T(8,128)(2,1)} %copy-done.2, bf16[128,8,512]{2,1,0:T(8,128)(2,1)} %copy-done.6, bf16[7,512,1024]{2,1,0:T(8,128)(2,1)S(1)} %bitcast.90), kind=kOutput, calls=%fused_computation.50 | convolution fusion | flops 1075838976 | bytes 7077888 | tf_op jit(solution)/shard_map/dot_general | solution.py:92
  80.4 3.3 %fusion.32 = f32[1024,1024]{1,0:T(8,128)} fusion(bf16[128,6,512]{2,1,0:T(8,128)(2,1)S(1)} %copy-done.3, bf16[128,8,512]{2,1,0:T(8,128)(2,1)S(1)} %copy-done.7, bf16[7,512,1024]{2,1,0:T(8,128)(2,1)S(1)} %bitcast.90), kind=kOutput, calls=%fused_computation.53 | convolution fusion | flops 1075838976 | bytes 7340032 | tf_op jit(solution)/shard_map/dot_general | solution.py:92
  83.7 0.7 fusion.34
  84.5 0.2 copy.42
  84.7 0.9 fusion.6
  85.6 0.5 pad_maximum_fusion.4
  86.1 1.2 %copy.43 = bf16[128,7,512]{2,0,1:T(8,128)(2,1)} copy(bf16[128,7,512]{2,1,0:T(8,128)(2,1)S(1)} %pad_maximum_fusion.4) | data formatting | bytes 1835008
  87.3 7.7 %fusion.4 = bf16[128,8,1024]{2,1,0:T(8,128)(2,1)} fusion(f32[1024,1024]{1,0:T(8,128)} %fusion.32, f32[1024,1024]{1,0:T(8,128)S(1)} %fusion.28, f32[1024,1024]{1,0:T(8,128)S(1)} %fusion.24, f32[1024,1024]{1,0:T(8,128)S(1)} %fusion.20, f32[1024,1024]{1,0:T(8,128)S(1)} %fusion.16, f32[1024,1024]{1,0:T(8,128)S(1)} %fusion.12, ...), kind=kOutput, calls=%fused_computation.8 | convolution fusion | flops 1086324736 | bytes 29365248 | tf_op jit(solution)/shard_map/dot_general | solution.py:92
  (60 shorter events, 1.7 us)
Async XLA Ops:
  0.6 13.2 %copy-start.8 = (bf16[128,7,512]{2,0,1:T(8,128)(2,1)S(1)}, bf16[128,7,512]{2,0,1:T(8,128)(2,1)}, u32[]{:S(2)}) copy-start(bf16[128,7,512]{2,0,1:T(8,128)(2,1)} %param.9) | copy-start | bytes 2752516
  4.8 14.1 %all-to-all-start = ((bf16[16,1,14]{2,1,0:T(2,128)(2,1)}), bf16[16,1,14]{2,1,0:T(2,128)(2,1)S(1)}, u32[]{:S(2)}, u32[]{:S(2)}) async-start(bf16[16,1,14]{2,1,0:T(2,128)(2,1)} %copy.36), calls=%async_computation | async-start | bytes 16384 | tf_op jit(solution)/shard_map/all_to_all | solution.py:71
  17.7 7.2 %copy-start.12 = (s32[128]{0:T(128)S(1)}, s32[128]{0:T(128)}, u32[]{:S(2)}) copy-start(s32[128]{0:T(128)} %param.12) | copy-start | bytes 1540
  17.7 7.2 %copy-start.10 = (f32[4,512]{1,0:T(4,128)S(1)}, f32[4,512]{1,0:T(4,128)}, u32[]{:S(2)}) copy-start(f32[4,512]{1,0:T(4,128)} %param.13) | copy-start | bytes 24580
  18.9 33.5 %all-to-all-start.1 = ((bf16[16,2,18176]{2,1,0:T(2,128)(2,1)}), bf16[16,2,18176]{2,1,0:T(2,128)(2,1)}, u32[]{:S(2)}, u32[]{:S(2)}) async-start(bf16[16,2,18176]{2,1,0:T(2,128)(2,1)} %reshape.155), calls=%async_computation.1 | async-start | bytes 2326528 | tf_op jit(solution)/shard_map/all_to_all | solution.py:70
  60.9 2.1 %copy-start = (bf16[128,4,512]{2,1,0:T(4,128)(2,1)}, bf16[128,4,512]{2,1,0:T(4,128)(2,1)S(1)}, u32[]{:S(2)}) copy-start(bf16[128,4,512]{2,1,0:T(4,128)(2,1)S(1)} %reshape.143) | copy-start | bytes 1572868
  61.1 1.9 %copy-start.4 = (bf16[128,1,512]{2,1,0:T(2,128)(2,1)}, bf16[128,1,512]{2,1,0:T(2,128)(2,1)S(1)}, u32[]{:S(2)}) copy-start(bf16[128,1,512]{2,1,0:T(2,128)(2,1)S(1)} %copy.40) | copy-start | bytes 393220
  66.7 9.4 %copy-start.6 = (bf16[128,8,512]{2,1,0:T(8,128)(2,1)}, bf16[128,8,512]{2,1,0:T(8,128)(2,1)S(1)}, u32[]{:S(2)}) copy-start(bf16[128,8,512]{2,1,0:T(8,128)(2,1)S(1)} %convert_element_type.124) | copy-start | bytes 3145732
  69.1 7.0 %copy-start.2 = (bf16[128,6,512]{2,1,0:T(8,128)(2,1)}, bf16[128,6,512]{2,1,0:T(8,128)(2,1)S(1)}, u32[]{:S(2)}) copy-start(bf16[128,6,512]{2,1,0:T(8,128)(2,1)S(1)} %copy.48) | copy-start | bytes 2359300
  69.1 5.6 %slice-start = ((s8[7340032]{0:T(1024)(128)(4,1)}), s8[4194304]{0:T(1024)(128)(4,1)S(1)}, s32[]{:S(2)}) async-start(s8[7340032]{0:T(1024)(128)(4,1)} %bitcast.89), calls=%async_computation.2 | async-start | bytes 8388608
  72.0 2.7 %slice-start.1 = ((s8[7340032]{0:T(1024)(128)(4,1)}), s8[3145728]{0:T(1024)(128)(4,1)S(1)}, s32[]{:S(2)}) async-start(s8[7340032]{0:T(1024)(128)(4,1)} %bitcast.89), calls=%async_computation.3 | async-start | bytes 6291456
  77.4 3.0 %copy-start.3 = (bf16[128,6,512]{2,1,0:T(8,128)(2,1)S(1)}, bf16[128,6,512]{2,1,0:T(8,128)(2,1)}, u32[]{:S(2)}) copy-start(bf16[128,6,512]{2,1,0:T(8,128)(2,1)} %copy-done.2) | copy-start | bytes 2359300
  77.4 3.0 %copy-start.7 = (bf16[128,8,512]{2,1,0:T(8,128)(2,1)S(1)}, bf16[128,8,512]{2,1,0:T(8,128)(2,1)}, u32[]{:S(2)}) copy-start(bf16[128,8,512]{2,1,0:T(8,128)(2,1)} %copy-done.6) | copy-start | bytes 3145732
  80.4 3.3 %copy-start.1 = (bf16[128,4,512]{2,1,0:T(4,128)(2,1)S(1)}, bf16[128,4,512]{2,1,0:T(4,128)(2,1)}, u32[]{:S(2)}) copy-start(bf16[128,4,512]{2,1,0:T(4,128)(2,1)} %copy-done) | copy-start | bytes 1572868
  80.4 3.3 %copy-start.5 = (bf16[128,1,512]{2,1,0:T(2,128)(2,1)S(1)}, bf16[128,1,512]{2,1,0:T(2,128)(2,1)}, u32[]{:S(2)}) copy-start(bf16[128,1,512]{2,1,0:T(2,128)(2,1)} %copy-done.4) | copy-start | bytes 393220
  83.7 1.0 %copy-start.9 = (s32[128,6]{1,0:T(8,128)S(1)}, s32[128,6]{1,0:T(8,128)}, u32[]{:S(2)}) copy-start(s32[128,6]{1,0:T(8,128)} %iota_add_fusion) | copy-start | bytes 9220
  85.5 1.8 %copy-start.11 = (f32[1024]{0:T(1024)S(1)}, f32[1024]{0:T(1024)}, u32[]{:S(2)}) copy-start(f32[1024]{0:T(1024)} %param.15) | copy-start | bytes 12292
where the time goes:
time: 95.5 us; the launch traced here: 95 us
  waiting for transfers between devices  26.3 us (28%)
  matrix products  26.2 us (27%)
  local copies, waits for them, and re-layouts  19 us (20%)
  starting transfers between devices  12.6 us (13%)
  other arithmetic  9.85 us (10%)
  between operations  1.2 us (1%)
    all_to_all x1, waiting for transfers between devices, body(): lax.all_to_all(joint, 'dec', split_axis=0, concat_axis=0, tiled=True)  26.3 us
    dot_general x7, matrix products, body(): jnp.dot(window, conv_weight[tap], preferred_element_type=jnp.float32)  22.2 us
    unnamed x38, local copies, waits for them, and re-layouts  9.72 us
    all_to_all x1, starting transfers between devices, body(): lax.all_to_all(joint_labels, 'dec', split_axis=0, concat_axis=0, tiled=True)  6.55 us
    all_to_all x1, starting transfers between devices, body(): lax.all_to_all(joint, 'dec', split_axis=0, concat_axis=0, tiled=True)  6.02 us
    convert_element_type x1, other arithmetic, body(): jnp.stack([even, odd], axis=2).reshape(streams, 2 * frames, channels)  2.43 us
  transfers between devices with their start and end apart: 2, of which 1 were waited for; matrix products, arithmetic and copies ran while one was open for 9% of the time, Pallas kernels for 0%

commit v1 on v0

v1 whole, which is shorter than its diff:
```python
import jax
import jax.numpy as jnp
from jax import lax
from jax.experimental import pallas as pl
from jax.experimental.pallas import tpu as pltpu
from jax.sharding import PartitionSpec as P


LABEL_WIDTH = 128


def buckets(rows, target, local, capacity, number):
    hits = (target[:, None] == jnp.arange(number, dtype=jnp.int32)[None, :]).astype(jnp.int32)
    rank = jnp.sum(hits * (jnp.cumsum(hits, axis=0) - 1), axis=1)
    place = jnp.where(target >= 0, target * capacity + rank, -1)
    picker = (place[:, None] == jnp.arange(number * capacity, dtype=jnp.int32)[None, :]).astype(
        jnp.bfloat16
    )
    packed = jnp.dot(picker.T, rows, preferred_element_type=jnp.float32).astype(jnp.bfloat16)
    labels = (
        jnp.sum(picker.T.astype(jnp.float32) * (local + 1).astype(jnp.float32)[None, :], axis=1)
        - 1.0
    )
    width = rows.shape[1]
    return (
        packed.reshape(number, capacity * width),
        labels.reshape(number, capacity),
    )


def settle(received, labels, streams):
    picker = (labels[:, None] == jnp.arange(streams, dtype=jnp.float32)[None, :]).astype(
        jnp.bfloat16
    )
    return jnp.dot(picker.T, received, preferred_element_type=jnp.float32)


def conv_kernel(ext_ref, w_ref, b_ref, lim_ref, o_ref):
    taps = w_ref.shape[0]
    steps, streams, block = o_ref.shape
    channels = ext_ref.shape[2]
    acc = None
    for tap in range(taps):
        window = ext_ref[tap : tap + steps].reshape(steps * streams, channels)
        part = jnp.dot(window, w_ref[tap], preferred_element_type=jnp.float32)
        acc = part if acc is None else acc + part
    acc = acc + b_ref[...]
    act = jnp.where(acc > 0, acc, jnp.exp(jnp.minimum(acc, 0.0)) - 1.0)
    act = act.reshape(steps, streams, block)
    lim = lim_ref[...]
    for step in range(steps):
        keep = step < lim
        o_ref[step] = jnp.where(keep, act[step], 0.0).astype(o_ref.dtype)


def conv_call(ext_t, conv_weight, conv_bias, limit, steps):
    rows, streams, channels = ext_t.shape
    taps, _, outward = conv_weight.shape
    block = 256 if outward % 256 == 0 else outward
    return pl.pallas_call(
        conv_kernel,
        out_shape=jax.ShapeDtypeStruct((steps, streams, outward), jnp.bfloat16),
        grid=(outward // block,),
        in_specs=[
            pl.BlockSpec((rows, streams, channels), lambda n: (0, 0, 0)),
            pl.BlockSpec((taps, channels, block), lambda n: (0, 0, n)),
            pl.BlockSpec((1, block), lambda n: (0, n)),
            pl.BlockSpec((streams, 1), lambda n: (0, 0)),
        ],
        out_specs=pl.BlockSpec((steps, streams, block), lambda n: (0, 0, n)),
    )(ext_t, conv_weight, conv_bias.reshape(1, outward), limit)


def body(latents, cache, panel_slot, cache_slot, frames_valid, up_weight, conv_weight, conv_bias):
    number = lax.axis_size("dec")
    myself = lax.axis_index("dec")
    streams = latents.shape[0]
    frames = latents.shape[1]
    channels = latents.shape[2]
    rows_kept = cache.shape[1]
    pair_cap = max(2, (streams + number - 2) // (number - 1))
    mig_cap = max(2, (streams // 2 + number - 3) // (number - 2))
    panel_width = frames * channels
    cache_width = rows_kept * channels
    flat_latents = latents.reshape(streams, panel_width)
    flat_cache = cache.reshape(streams, cache_width)
    panel_owner = panel_slot // streams
    panel_local = panel_slot % streams
    cache_owner = cache_slot // streams
    cache_local = cache_slot % streams
    moving = cache_owner != myself
    staying = jnp.logical_not(moving)
    stay_pick = (
        staying[:, None] & (cache_local[:, None] == jnp.arange(streams, dtype=jnp.int32)[None, :])
    ).astype(jnp.bfloat16)
    kept = jnp.dot(stay_pick.T, flat_cache, preferred_element_type=jnp.float32)
    cache_send, cache_labels = buckets(
        flat_cache, jnp.where(moving, cache_owner, -1), cache_local, mig_cap, number
    )
    panel_send, panel_labels = buckets(flat_latents, panel_owner, panel_local, pair_cap, number)
    label_block = jnp.concatenate([panel_labels, cache_labels], axis=1)
    label_block = jnp.pad(
        label_block, ((0, 0), (0, LABEL_WIDTH - label_block.shape[1])), constant_values=-1.0
    ).astype(jnp.bfloat16)
    joint = jnp.concatenate([panel_send, cache_send, label_block], axis=1)
    joint_recv = lax.all_to_all(joint, "dec", split_axis=0, concat_axis=0, tiled=True)
    split_at = pair_cap * panel_width
    label_at = split_at + mig_cap * cache_width
    panel_recv = joint_recv[:, :split_at].reshape(number * pair_cap, panel_width)
    cache_recv = joint_recv[:, split_at:label_at].reshape(number * mig_cap, cache_width)
    recv_labels = joint_recv[:, label_at:].astype(jnp.float32)
    panel_rl = recv_labels[:, :pair_cap].reshape(-1)
    cache_rl = recv_labels[:, pair_cap : pair_cap + mig_cap].reshape(-1)
    panels = settle(panel_recv, panel_rl, streams)
    arrived = settle(cache_recv, cache_rl, streams)
    latent_rows = panels.astype(jnp.bfloat16).reshape(streams, frames, channels)
    owned = (kept + arrived).astype(jnp.bfloat16).reshape(streams, rows_kept, channels)
    previous = jnp.concatenate([owned[:, 0:1], latent_rows], axis=1)
    previous_t = jnp.transpose(previous, (1, 0, 2))
    current = previous_t[1:].astype(jnp.float32)
    earlier = previous_t[:-1].astype(jnp.float32)
    even = up_weight[0] * current + up_weight[2] * earlier
    odd = up_weight[1] * current + up_weight[3] * earlier
    upsampled_t = (
        jnp.stack([even, odd], axis=1).reshape(2 * frames, streams, channels).astype(jnp.bfloat16)
    )
    owned_t = jnp.transpose(owned[:, 1:], (1, 0, 2))
    extended_t = jnp.concatenate([owned_t, upsampled_t], axis=0)
    limit = (2 * frames_valid).reshape(streams, 1)
    decoded_t = conv_call(extended_t, conv_weight, conv_bias, limit, 2 * frames)
    decoded = jnp.transpose(decoded_t, (1, 0, 2))
    taps = conv_weight.shape[0]
    last_latent = previous[:, 1]
    last_rows = extended_t[2 : 2 + taps - 1]
    for valid in range(2, frames + 1):
        chosen = frames_valid == valid
        last_latent = jnp.where(chosen[:, None], previous[:, valid], last_latent)
        last_rows = jnp.where(
            chosen[None, :, None], extended_t[2 * valid : 2 * valid + taps - 1], last_rows
        )
    new_cache = jnp.concatenate(
        [last_latent[:, None], jnp.transpose(last_rows, (1, 0, 2))], axis=1
    )
    return (decoded, new_cache)


def solution(mesh):
    in_specs = (
        P(("grp", "dec"), None, None),
        P(("grp", "dec"), None, None),
        P(("grp", "dec")),
        P(("grp", "dec")),
        P(("grp", "dec")),
        P(),
        P(),
        P(),
    )
    out_specs = (P(("grp", "dec"), None, None), P(("grp", "dec"), None, None))
    return jax.shard_map(body, mesh=mesh, in_specs=in_specs, out_specs=out_specs, check_vma=False)
```

time: 95.5 us -> 85.7 us (0.90)
  matrix products: 26.2 us -> 2.4 us
  Pallas kernels: 0 us -> 11.6 us
  local copies, waits for them, and re-layouts: 19 us -> 27.1 us
  starting transfers between devices: 12.6 us -> 6.56 us
    dot_general x11 -> x2, matrix products: 24.7 us -> 0.92 us  [settle(): return jnp.dot(picker.T, received, preferred_element_type=jnp.float32)]
    pallas_call x0 -> x1, Pallas kernels: none -> 11.6 us  [conv_call(): pl.pallas_call(conv_kernel, out_shape=jax.ShapeDtypeStruct((steps, stream...]
    unnamed x38 -> x25, local copies, waits for them, and re-layouts: 9.72 us -> 17.2 us
    all_to_all x1 -> x0, starting transfers between devices: 6.55 us -> none  [body(): lax.all_to_all(joint_labels, 'dec', split_axis=0, concat_axis=0, tiled=True)]
    another operation x6 -> x1, local copies, waits for them, and re-layouts: 4.46 us -> 0.53 us  [body(): jnp.stack([even, odd], axis=1).reshape(2 * frames, streams, channels)]
    slice x3 -> x7, local copies, waits for them, and re-layouts: 0.13 us -> 3.93 us  [the longest x2 2.81 us: body(): extended_t[2 * valid:2 * valid + taps - 1]]
    reshape x1 -> x5, local copies, waits for them, and re-layouts: 0.38 us -> 3.62 us  [the longest x2 1.45 us: buckets(): packed.reshape(number, capacity * width)]
    convert_element_type x5 -> x1, other arithmetic: 2.53 us -> 0.01 us  [body(): recv_labels = joint_recv[:, label_at:].astype(jnp.float32)]
  transfers between devices with their start and end apart: 2 -> 1, of which waited for: 1 -> 1; matrix products, arithmetic and copies ran while one was open for 9% -> 1% of each run, Pallas kernels for 0% -> 0%
where the time goes in v1:
time: 85.7 us; the launch traced here: 85.2 us
  local copies, waits for them, and re-layouts  27.1 us (32%)
  waiting for transfers between devices  26.9 us (31%)
  Pallas kernels  11.6 us (14%)
  other arithmetic  9.65 us (11%)
  starting transfers between devices  6.56 us (8%)
  matrix products  2.4 us (3%)
  between operations  1 us (1%)
    all_to_all x1, waiting for transfers between devices, body(): lax.all_to_all(joint, 'dec', split_axis=0, concat_axis=0, tiled=True)  26.9 us
    unnamed x25, local copies, waits for them, and re-layouts  17.2 us
    pallas_call x1, Pallas kernels, conv_call(): pl.pallas_call(conv_kernel, out_shape=jax.ShapeDtypeStruct((steps, stream...  11.6 us
    all_to_all x1, starting transfers between devices, body(): lax.all_to_all(joint, 'dec', split_axis=0, concat_axis=0, tiled=True)  6.56 us
    slice x2, local copies, waits for them, and re-layouts, body(): extended_t[2 * valid:2 * valid + taps - 1]  2.81 us
    another operation x3, other arithmetic, body(): jnp.stack([even, odd], axis=1).reshape(2 * frames, streams, channels)  1.75 us
  transfers between devices with their start and end apart: 1, of which 1 were waited for; matrix products, arithmetic and copies ran while one was open for 1% of the time, Pallas kernels for 0%

profile of v1, /device:TPU:13, one launch (start us, length us, event | category | flops | bytes accessed | tf_op | source)
XLA Modules:
  0.0 85.2 jit_solution(6323641274865634949)
XLA Ops:
  0.6 0.7 and_select_fusion.1
  1.3 0.7 compare_not_fusion
  2.1 0.2 reduce_window_sum.18
  2.2 0.2 select_reduce_fusion
  2.4 0.8 add_convert_fusion.2
  3.2 0.1 multiply_reduce_fusion.1
  3.5 0.2 reduce_window_sum.17
  3.7 0.2 select_reduce_fusion.1
  3.9 0.1 multiply_reduce_fusion
  4.1 1.2 %copy.72 = bf16[16,8,4,512]{3,1,2,0:T(8,128)(2,1)S(1)} copy(bf16[16,8,4,512]{3,2,1,0:T(4,128)(2,1)} %bitcast.53) | data formatting | bytes 1048576
  5.2 0.4 convolution_convert_fusion.1
  5.7 0.9 %reshape.87 = bf16[16,18432]{1,0:T(8,128)(2,1)S(1)} reshape(bf16[144,2048]{1,0:T(8,128)(2,1)S(1)} %convolution_convert_fusion.1) | data formatting | bytes 1179648 | tf_op jit(solution)/shard_map/reshape | solution.py:26
  6.6 0.6 copy.52
  7.2 0.5 convolution_convert_fusion
  7.7 0.6 reshape.88
  8.5 0.5 broadcast.130
  9.0 1.5 %reduce = bf16[16,36480]{1,0:T(8,128)(2,1)S(1)} reduce(bf16[16,1,36480]{2,0,1:T(8,128)(2,1)S(1)} %maximum_bitcast_fusion, bf16[]{:T(256)} %broadcast.130), dimensions={1}, to_apply=%copy.53.reduce_sub_computation | reduce | bytes 2334722 | tf_op jit(solution)/shard_map/all_to_all | solution.py:106
  10.5 1.7 %reshape.95 = bf16[16,2,18240]{2,1,0:T(2,128)(2,1)} reshape(bf16[16,36480]{1,0:T(8,128)(2,1)S(1)} %reduce) | data formatting | bytes 2334720
  12.2 6.6 %all-to-all-start = ((bf16[16,2,18240]{2,1,0:T(2,128)(2,1)}), bf16[16,2,18240]{2,1,0:T(2,128)(2,1)}, u32[]{:S(2)}, u32[]{:S(2)}) async-start(bf16[16,2,18240]{2,1,0:T(2,128)(2,1)} %reshape.95), calls=%async_computation | async-start | bytes 2342912 | tf_op jit(solution)/shard_map/all_to_all | solution.py:106
  18.8 0.7 copy.58.lim_ref
  19.6 26.9 %all-to-all-done = bf16[16,2,18240]{2,1,0:T(2,128)(2,1)} async-done(((bf16[16,2,18240]{2,1,0:T(2,128)(2,1)}), bf16[16,2,18240]{2,1,0:T(2,128)(2,1)}, u32[]{:S(2)}, u32[]{:S(2)}) %all-to-all-start) | async-done | bytes 1167392 | tf_op jit(solution)/shard_map/all_to_all | solution.py:106
  46.5 6.2 %reshape.96 = bf16[16,1,36480]{2,1,0:T(2,128)(2,1)S(1)} reshape(bf16[16,2,18240]{2,1,0:T(2,128)(2,1)} %all-to-all-done) | data formatting | bytes 2334720
  52.7 0.1 copy.74
  53.2 0.6 reshape.89
  53.7 0.5 fusion.23
  54.2 0.5 fusion
  54.8 0.6 copy.54
  55.4 0.9 %slice.95 = bf16[128,6,512]{0,2,1:T(8,128)(2,1)} slice(bf16[128,7,512]{0,2,1:T(8,128)(2,1)S(1)} %bitcast.51), slice={[0:128], [1:7], [0:512]} | slice | bytes 1572864 | tf_op jit(solution)/shard_map/slice | solution.py:127
  56.4 0.9 %reshape.91 = bf16[144,2048]{1,0:T(8,128)(2,1)S(1)} reshape(bf16[16,18432]{1,0:T(8,128)(2,1)S(1)} %slice.98) | data formatting | bytes 1179648 | tf_op jit(solution)/shard_map/reshape | solution.py:109
  57.3 0.4 convolution_convert_fusion.2
  57.7 0.3 copy.56
  58.1 0.4 fusion.14
  58.7 1.2 %fusion.5 = (bf16[3,2,128,512]{2,3,0,1:T(8,128)(2,1)}, bf16[3,2,128,512]{2,3,0,1:T(8,128)(2,1)}) fusion(bf16[4,1,128,512]{2,3,0,1:T(8,128)(2,1)S(1)} %get-tuple-element.18, bf16[4,1,128,512]{2,3,0,1:T(8,128)(2,1)S(1)} %get-tuple-element.19), kind=kLoop, calls=%fused_computation.26 | loop fusion | flops 786432 | bytes 2621440 | tf_op jit(solution)/shard_map/stack | solution.py:125
  59.9 0.1 copy.71
  60.0 0.8 copy.70
  60.8 0.8 copy.69
  61.5 0.8 copy.68
  62.3 0.3 copy.67
  62.6 0.5 copy.57
  63.1 1.4 %copy.63 = bf16[3,2,128,512]{3,2,1,0:T(8,128)(2,1)S(1)} copy(bf16[3,2,128,512]{2,3,0,1:T(8,128)(2,1)} %get-tuple-element.16) | data formatting | bytes 1572864 | tf_op jit(solution)/shard_map/slice | solution.py:139
  64.6 1.4 %copy.64 = bf16[3,2,128,512]{3,2,1,0:T(8,128)(2,1)S(1)} copy(bf16[3,2,128,512]{2,3,0,1:T(8,128)(2,1)} %get-tuple-element.17) | data formatting | bytes 1572864 | tf_op jit(solution)/shard_map/slice | solution.py:139
  66.0 1.4 %pad_maximum_fusion.ext_ref = bf16[14,128,512]{2,1,0:T(8,128)(2,1)} fusion(bf16[6,128,512]{2,1,0:T(8,128)(2,1)S(1)} %bitcast.43, bf16[8,128,512]{2,1,0:T(8,128)(2,1)S(1)} %bitcast.38), kind=kLoop, calls=%fused_computation.5 | loop fusion | flops 917504 | bytes 3670016 | tf_op jit(solution)/shard_map/concatenate | solution.py:128
  67.4 11.6 %shard_map.95 = bf16[8,128,1024]{2,1,0:T(8,128)(2,1)} custom-call(bf16[14,128,512]{2,1,0:T(8,128)(2,1)} %pad_maximum_fusion.ext_ref, bf16[7,512,1024]{2,1,0:T(8,128)(2,1)} %w_ref.1, f32[1,1024]{1,0:T(1,128)} %bitcast.59, s32[128,1]{1,0:T(8,128)} %copy.58.lim_ref), custom_call_target="tpu_custom_call" | custom-call | tf_op jit(solution)/shard_map/pallas_call | solution.py:60
  78.9 4.1 %copy.65 = bf16[128,8,1024]{2,1,0:T(8,128)(2,1)} copy(bf16[128,8,1024]{2,0,1:T(8,128)(2,1)} %bitcast.40) | data formatting | bytes 4194304
  83.0 0.4 fusion.11
  83.4 0.5 copy-done.2
  84.0 0.1 select_select_fusion
  84.2 1.0 %pad_maximum_fusion.2 = bf16[128,7,512]{2,0,1:T(8,128)(2,1)} fusion(bf16[128,6,512]{2,0,1:T(8,128)(2,1)S(1)} %fusion.11, bf16[128,1,512]{2,0,1:T(8,128)(2,1)S(1)} %select_select_fusion), kind=kLoop, calls=%fused_computation.25 | loop fusion | flops 458752 | bytes 1835008 | tf_op jit(solution)/shard_map/concatenate | solution.py:141
  (36 shorter events, 1.2 us)
Async XLA Ops:
  2.4 4.1 %copy-start.1 = (bf16[128,7,512]{2,0,1:T(8,128)(2,1)S(1)}, bf16[128,7,512]{2,0,1:T(8,128)(2,1)}, u32[]{:S(2)}) copy-start(bf16[128,7,512]{2,0,1:T(8,128)(2,1)} %param.9) | copy-start | bytes 2752516
  10.5 8.3 %copy-start.6 = (s32[128]{0:T(128)S(1)}, s32[128]{0:T(128)}, u32[]{:S(2)}) copy-start(s32[128]{0:T(128)} %param.12) | copy-start | bytes 1540
  10.5 9.0 %copy-start.5 = (f32[4,512]{1,0:T(4,128)S(1)}, f32[4,512]{1,0:T(4,128)}, u32[]{:S(2)}) copy-start(f32[4,512]{1,0:T(4,128)} %param.13) | copy-start | bytes 24580
  12.2 34.2 %all-to-all-start = ((bf16[16,2,18240]{2,1,0:T(2,128)(2,1)}), bf16[16,2,18240]{2,1,0:T(2,128)(2,1)}, u32[]{:S(2)}, u32[]{:S(2)}) async-start(bf16[16,2,18240]{2,1,0:T(2,128)(2,1)} %reshape.95), calls=%async_computation | async-start | bytes 2342912 | tf_op jit(solution)/shard_map/all_to_all | solution.py:106
  58.6 3.7 %copy-start = (bf16[128,6,512]{0,2,1:T(8,128)(2,1)S(1)}, bf16[128,6,512]{0,2,1:T(8,128)(2,1)}, u32[]{:S(2)}) copy-start(bf16[128,6,512]{0,2,1:T(8,128)(2,1)} %slice.95) | copy-start | bytes 2359300
  83.0 0.9 %copy-start.2 = (bf16[128,1,512]{2,0,1:T(8,128)(2,1)S(1)}, bf16[128,1,512]{2,0,1:T(8,128)(2,1)}, u32[]{:S(2)}) copy-start(bf16[128,1,512]{2,0,1:T(8,128)(2,1)} %copy.70) | copy-start | bytes 393220
  83.0 1.0 %copy-start.3 = (bf16[128,1,512]{2,0,1:T(8,128)(2,1)S(1)}, bf16[128,1,512]{2,0,1:T(8,128)(2,1)}, u32[]{:S(2)}) copy-start(bf16[128,1,512]{2,0,1:T(8,128)(2,1)} %copy.69) | copy-start | bytes 393220
  83.0 1.0 %copy-start.4 = (bf16[128,1,512]{2,0,1:T(8,128)(2,1)S(1)}, bf16[128,1,512]{2,0,1:T(8,128)(2,1)}, u32[]{:S(2)}) copy-start(bf16[128,1,512]{2,0,1:T(8,128)(2,1)} %copy.68) | copy-start | bytes 393220

commit v2 on v1

--- a/solution.py
+++ b/solution.py
@@ -1,3 +1,5 @@
+import functools
+
 import jax
 import jax.numpy as jnp
 from jax import lax
@@ -32,34 +34,42 @@
     picker = (labels[:, None] == jnp.arange(streams, dtype=jnp.float32)[None, :]).astype(
         jnp.bfloat16
     )
-    return jnp.dot(picker.T, received, preferred_element_type=jnp.float32)
+    return jnp.einsum("ps,pqc->sqc", picker, received, preferred_element_type=jnp.float32)
 
 
-def conv_kernel(ext_ref, w_ref, b_ref, lim_ref, o_ref):
+def conv_kernel(ext_ref, w_ref, b_ref, lim_ref, o_ref, *, group):
     taps = w_ref.shape[0]
-    steps, streams, block = o_ref.shape
+    streams, steps, block = o_ref.shape
     channels = ext_ref.shape[2]
-    acc = None
-    for tap in range(taps):
-        window = ext_ref[tap : tap + steps].reshape(steps * streams, channels)
-        part = jnp.dot(window, w_ref[tap], preferred_element_type=jnp.float32)
-        acc = part if acc is None else acc + part
-    acc = acc + b_ref[...]
-    act = jnp.where(acc > 0, acc, jnp.exp(jnp.minimum(acc, 0.0)) - 1.0)
-    act = act.reshape(steps, streams, block)
-    lim = lim_ref[...]
-    for step in range(steps):
-        keep = step < lim
-        o_ref[step] = jnp.where(keep, act[step], 0.0).astype(o_ref.dtype)
+    rows = steps * group
+    line = lax.broadcasted_iota(jnp.int32, (rows, rows), 0)
+    column = lax.broadcasted_iota(jnp.int32, (rows, rows), 1)
+    order = ((line // steps) == (column % group)) & ((line % steps) == (column // group))
+    order = order.astype(jnp.bfloat16)
+    position = lax.broadcasted_iota(jnp.int32, (steps, group, 1), 0)
+    for first in range(0, streams, group):
+        acc = None
+        for tap in range(taps):
+            window = ext_ref[tap : tap + steps, first : first + group, :].reshape(rows, channels)
+            part = jnp.dot(window, w_ref[tap], preferred_element_type=jnp.float32)
+            acc = part if acc is None else acc + part
+        acc = acc + b_ref[...]
+        act = jnp.where(acc > 0, acc, jnp.exp(jnp.minimum(acc, 0.0)) - 1.0)
+        act = act.reshape(steps, group, block)
+        keep = position < lim_ref[first : first + group, :][None]
+        act = jnp.where(keep, act, 0.0).astype(jnp.bfloat16).reshape(rows, block)
+        moved = jnp.dot(order, act, preferred_element_type=jnp.float32)
+        o_ref[first : first + group] = moved.reshape(group, steps, block).astype(o_ref.dtype)
 
 
 def conv_call(ext_t, conv_weight, conv_bias, limit, steps):
     rows, streams, channels = ext_t.shape
     taps, _, outward = conv_weight.shape
     block = 256 if outward % 256 == 0 else outward
+    group = 32 if streams % 32 == 0 else streams
     return pl.pallas_call(
-        conv_kernel,
-        out_shape=jax.ShapeDtypeStruct((steps, streams, outward), jnp.bfloat16),
+        functools.partial(conv_kernel, group=group),
+        out_shape=jax.ShapeDtypeStruct((streams, steps, outward), jnp.bfloat16),
         grid=(outward // block,),
         in_specs=[
             pl.BlockSpec((rows, streams, channels), lambda n: (0, 0, 0)),
@@ -67,7 +77,7 @@
             pl.BlockSpec((1, block), lambda n: (0, n)),
             pl.BlockSpec((streams, 1), lambda n: (0, 0)),
         ],
-        out_specs=pl.BlockSpec((steps, streams, block), lambda n: (0, 0, n)),
+        out_specs=pl.BlockSpec((streams, steps, block), lambda n: (0, 0, n)),
     )(ext_t, conv_weight, conv_bias.reshape(1, outward), limit)
 
 
@@ -98,21 +108,32 @@
         flat_cache, jnp.where(moving, cache_owner, -1), cache_local, mig_cap, number
     )
     panel_send, panel_labels = buckets(flat_latents, panel_owner, panel_local, pair_cap, number)
+    lane = LABEL_WIDTH
+    panel_rows = pair_cap * panel_width // lane
+    cache_rows = mig_cap * cache_width // lane
+    label_rows = -(panel_rows + cache_rows + 1) % 16 + 1
     label_block = jnp.concatenate([panel_labels, cache_labels], axis=1)
     label_block = jnp.pad(
-        label_block, ((0, 0), (0, LABEL_WIDTH - label_block.shape[1])), constant_values=-1.0
+        label_block, ((0, 0), (0, label_rows * lane - label_block.shape[1])), constant_values=-1.0
     ).astype(jnp.bfloat16)
-    joint = jnp.concatenate([panel_send, cache_send, label_block], axis=1)
+    joint = jnp.concatenate(
+        [
+            panel_send.reshape(number, panel_rows, lane),
+            cache_send.reshape(number, cache_rows, lane),
+            label_block.reshape(number, label_rows, lane),
+        ],
+        axis=1,
+    )
     joint_recv = lax.all_to_all(joint, "dec", split_axis=0, concat_axis=0, tiled=True)
-    split_at = pair_cap * panel_width
-    label_at = split_at + mig_cap * cache_width
-    panel_recv = joint_recv[:, :split_at].reshape(number * pair_cap, panel_width)
-    cache_recv = joint_recv[:, split_at:label_at].reshape(number * mig_cap, cache_width)
-    recv_labels = joint_recv[:, label_at:].astype(jnp.float32)
+    panel_recv = joint_recv[:, :panel_rows].reshape(number * pair_cap, panel_width // lane, lane)
+    cache_recv = joint_recv[:, panel_rows : panel_rows + cache_rows].reshape(
+        number * mig_cap, cache_width // lane, lane
+    )
+    recv_labels = joint_recv[:, panel_rows + cache_rows, :].astype(jnp.float32)
     panel_rl = recv_labels[:, :pair_cap].reshape(-1)
     cache_rl = recv_labels[:, pair_cap : pair_cap + mig_cap].reshape(-1)
-    panels = settle(panel_recv, panel_rl, streams)
-    arrived = settle(cache_recv, cache_rl, streams)
+    panels = settle(panel_recv, panel_rl, streams).reshape(streams, panel_width)
+    arrived = settle(cache_recv, cache_rl, streams).reshape(streams, cache_width)
     latent_rows = panels.astype(jnp.bfloat16).reshape(streams, frames, channels)
     owned = (kept + arrived).astype(jnp.bfloat16).reshape(streams, rows_kept, channels)
     previous = jnp.concatenate([owned[:, 0:1], latent_rows], axis=1)
@@ -127,8 +148,7 @@
     owned_t = jnp.transpose(owned[:, 1:], (1, 0, 2))
     extended_t = jnp.concatenate([owned_t, upsampled_t], axis=0)
     limit = (2 * frames_valid).reshape(streams, 1)
-    decoded_t = conv_call(extended_t, conv_weight, conv_bias, limit, 2 * frames)
-    decoded = jnp.transpose(decoded_t, (1, 0, 2))
+    decoded = conv_call(extended_t, conv_weight, conv_bias, limit, 2 * frames)
     taps = conv_weight.shape[0]
     last_latent = previous[:, 1]
     last_rows = extended_t[2 : 2 + taps - 1]

time: 85.7 us -> 80.8 us (0.943)
  local copies, waits for them, and re-layouts: 27.1 us -> 12.6 us
  Pallas kernels: 11.6 us -> 21.8 us
    unnamed x25 -> x21, local copies, waits for them, and re-layouts: 17.2 us -> 5.06 us
    pallas_call x1, Pallas kernels: 11.6 us -> 21.8 us  [conv_call(): pl.pallas_call(functools.partial(conv_kernel, group=group), out_shape=jax...]
    reshape x4 -> x2, local copies, waits for them, and re-layouts: 2.89 us -> 0.11 us  [the longest x1 0.09 us: body(): joint_recv[:, panel_rows:panel_rows + cache_rows]]
    all_to_all x2 -> x0, other arithmetic: 1.61 us -> none  [body(): lax.all_to_all(joint, 'dec', split_axis=0, concat_axis=0, tiled=True)]
    concatenate x0 -> x1, other arithmetic: none -> 1.1 us  [body(): jnp.concatenate([panel_send.reshape(number, panel_rows, lane), cache_send...]
    another operation x0 -> x2, local copies, waits for them, and re-layouts: none -> 1.02 us  [the longest x1 0.75 us: body(): cache_send.reshape(number, cache_rows, lane)]
where the time goes in v2:
time: 80.8 us; the launch traced here: 80.4 us
  waiting for transfers between devices  27 us (33%)
  Pallas kernels  21.8 us (27%)
  local copies, waits for them, and re-layouts  12.6 us (16%)
  other arithmetic  9.09 us (11%)
  starting transfers between devices  6.56 us (8%)
  matrix products  2.4 us (3%)
  between operations  0.97 us (1%)
    all_to_all x1, waiting for transfers between devices, body(): lax.all_to_all(joint, 'dec', split_axis=0, concat_axis=0, tiled=True)  27 us
    pallas_call x1, Pallas kernels, conv_call(): pl.pallas_call(functools.partial(conv_kernel, group=group), out_shape=jax...  21.8 us
    all_to_all x1, starting transfers between devices, body(): lax.all_to_all(joint, 'dec', split_axis=0, concat_axis=0, tiled=True)  6.56 us
    unnamed x21, local copies, waits for them, and re-layouts  5.06 us
    slice x2, local copies, waits for them, and re-layouts, body(): extended_t[2 * valid:2 * valid + taps - 1]  2.81 us
    another operation x3, other arithmetic, body(): jnp.stack([even, odd], axis=1).reshape(2 * frames, streams, channels)  1.75 us
  transfers between devices with their start and end apart: 1, of which 1 were waited for; matrix products, arithmetic and copies ran while one was open for 1% of the time, Pallas kernels for 0%

profile of v2, /device:TPU:13, one launch (start us, length us, event | category | flops | bytes accessed | tf_op | source)
XLA Modules:
  0.0 80.4 jit_solution(7803225455051926389)
XLA Ops:
  0.6 0.7 and_select_fusion.1
  1.3 0.7 compare_not_fusion
  2.1 0.2 reduce_window_sum.18
  2.2 0.2 select_reduce_fusion
  2.4 0.7 add_convert_fusion.2
  3.1 0.1 multiply_reduce_fusion.1
  3.2 0.1 sub.35
  3.3 0.1 fusion.23
  3.4 0.2 reduce_window_sum.17
  3.6 0.2 select_reduce_fusion.1
  3.8 0.1 multiply_reduce_fusion
  3.9 0.1 sub.33
  4.1 1.1 %copy.42 = bf16[16,8,4,512]{3,1,2,0:T(8,128)(2,1)S(1)} copy(bf16[16,8,4,512]{3,2,1,0:T(4,128)(2,1)} %bitcast.60) | data formatting | bytes 1048576
  5.3 0.4 convolution_convert_fusion.1
  5.7 0.3 reshape_reshape.6
  6.0 0.6 copy.25
  6.6 0.5 convolution_convert_fusion
  7.1 0.7 reshape_reshape.7
  7.9 1.1 %pad_maximum_fusion.2 = bf16[16,288,128]{2,1,0:T(8,128)(2,1)} fusion(bf16[16,4,128]{2,1,0:T(4,128)(2,1)S(1)} %reshape.88, bf16[16,140,128]{2,1,0:T(8,128)(2,1)S(1)} %reshape_reshape.7, bf16[16,144,128]{2,1,0:T(8,128)(2,1)S(1)} %reshape_reshape.6), kind=kLoop, calls=%fused_computation.19 | loop fusion | flops 3538944 | bytes 2359296 | tf_op jit(solution)/shard_map/concatenate | solution.py:119
  9.0 6.6 %all-to-all-start = ((bf16[16,288,128]{2,1,0:T(8,128)(2,1)}), bf16[16,288,128]{2,1,0:T(8,128)(2,1)S(1)}, u32[]{:S(2)}, u32[]{:S(2)}) async-start(bf16[16,288,128]{2,1,0:T(8,128)(2,1)} %pad_maximum_fusion.2), calls=%async_computation | async-start | bytes 2359296 | tf_op jit(solution)/shard_map/all_to_all | solution.py:127
  15.6 0.7 copy.30.lim_ref
  16.3 27.0 %all-to-all-done = bf16[16,288,128]{2,1,0:T(8,128)(2,1)S(1)} async-done(((bf16[16,288,128]{2,1,0:T(8,128)(2,1)}), bf16[16,288,128]{2,1,0:T(8,128)(2,1)S(1)}, u32[]{:S(2)}, u32[]{:S(2)}) %all-to-all-start) | async-done | bytes 1179680 | tf_op jit(solution)/shard_map/all_to_all | solution.py:127
  43.4 0.1 eq.148
  43.5 0.1 reshape.89
  43.6 0.5 fusion.15
  44.2 0.5 fusion
  44.7 0.6 copy.26
  45.3 0.9 %slice.95 = bf16[128,6,512]{0,2,1:T(8,128)(2,1)} slice(bf16[128,7,512]{0,2,1:T(8,128)(2,1)S(1)} %bitcast.56), slice={[0:128], [1:7], [0:512]} | slice | bytes 1572864 | tf_op jit(solution)/shard_map/slice | solution.py:148
  46.3 0.1 eq.152
  46.4 0.4 convolution_convert_fusion.2
  46.8 0.3 copy.28
  47.2 0.4 fusion.19
  47.6 0.1 pad_maximum_fusion.1
  47.7 1.2 %fusion.5 = (bf16[3,2,128,512]{2,3,0,1:T(8,128)(2,1)}, bf16[3,2,128,512]{2,3,0,1:T(8,128)(2,1)}) fusion(bf16[4,1,128,512]{2,3,0,1:T(8,128)(2,1)S(1)} %get-tuple-element.8, bf16[4,1,128,512]{2,3,0,1:T(8,128)(2,1)S(1)} %get-tuple-element.9), kind=kLoop, calls=%fused_computation.25 | loop fusion | flops 786432 | bytes 2621440 | tf_op jit(solution)/shard_map/stack | solution.py:146
  49.0 0.1 copy.41
  49.1 0.8 copy.40
  49.9 0.8 copy.39
  50.7 0.8 copy.38
  51.4 0.3 copy.37
  51.7 0.5 copy.29
  52.2 1.4 %copy.35 = bf16[3,2,128,512]{3,2,1,0:T(8,128)(2,1)S(1)} copy(bf16[3,2,128,512]{2,3,0,1:T(8,128)(2,1)} %get-tuple-element.6) | data formatting | bytes 1572864 | tf_op jit(solution)/shard_map/slice | solution.py:159
  53.6 1.4 %copy.36 = bf16[3,2,128,512]{3,2,1,0:T(8,128)(2,1)S(1)} copy(bf16[3,2,128,512]{2,3,0,1:T(8,128)(2,1)} %get-tuple-element.7) | data formatting | bytes 1572864 | tf_op jit(solution)/shard_map/slice | solution.py:159
  55.1 1.4 %pad_maximum_fusion.ext_ref = bf16[14,128,512]{2,1,0:T(8,128)(2,1)} fusion(bf16[6,128,512]{2,1,0:T(8,128)(2,1)S(1)} %bitcast.51, bf16[8,128,512]{2,1,0:T(8,128)(2,1)S(1)} %bitcast.47), kind=kLoop, calls=%fused_computation.5 | loop fusion | flops 917504 | bytes 3670016 | tf_op jit(solution)/shard_map/concatenate | solution.py:149
  56.5 0.4 fusion.11
  56.9 0.5 copy-done.2
  57.5 0.1 select_select_fusion
  57.6 1.0 %pad_maximum_fusion.3 = bf16[128,7,512]{2,0,1:T(8,128)(2,1)} fusion(bf16[128,6,512]{2,0,1:T(8,128)(2,1)S(1)} %fusion.11, bf16[128,1,512]{2,0,1:T(8,128)(2,1)S(1)} %select_select_fusion), kind=kLoop, calls=%fused_computation.24 | loop fusion | flops 458752 | bytes 1835008 | tf_op jit(solution)/shard_map/concatenate | solution.py:161
  58.6 21.8 %shard_map.95 = bf16[128,8,1024]{2,1,0:T(8,128)(2,1)} custom-call(bf16[14,128,512]{2,1,0:T(8,128)(2,1)} %pad_maximum_fusion.ext_ref, bf16[7,512,1024]{2,1,0:T(8,128)(2,1)} %w_ref.1, f32[1,1024]{1,0:T(1,128)} %bitcast.67, s32[128,1]{1,0:T(8,128)} %copy.30.lim_ref), custom_call_target="tpu_custom_call" | custom-call | tf_op jit(solution)/shard_map/pallas_call | solution.py:70
  (30 shorter events, 0.6 us)
Async XLA Ops:
  3.3 2.6 %copy-start.1 = (bf16[128,7,512]{2,0,1:T(8,128)(2,1)S(1)}, bf16[128,7,512]{2,0,1:T(8,128)(2,1)}, u32[]{:S(2)}) copy-start(bf16[128,7,512]{2,0,1:T(8,128)(2,1)} %param.9) | copy-start | bytes 2752516
  7.9 7.7 %copy-start.6 = (s32[128]{0:T(128)S(1)}, s32[128]{0:T(128)}, u32[]{:S(2)}) copy-start(s32[128]{0:T(128)} %param.12) | copy-start | bytes 1540
  7.9 8.4 %copy-start.5 = (f32[4,512]{1,0:T(4,128)S(1)}, f32[4,512]{1,0:T(4,128)}, u32[]{:S(2)}) copy-start(f32[4,512]{1,0:T(4,128)} %param.13) | copy-start | bytes 24580
  9.0 34.3 %all-to-all-start = ((bf16[16,288,128]{2,1,0:T(8,128)(2,1)}), bf16[16,288,128]{2,1,0:T(8,128)(2,1)S(1)}, u32[]{:S(2)}, u32[]{:S(2)}) async-start(bf16[16,288,128]{2,1,0:T(8,128)(2,1)} %pad_maximum_fusion.2), calls=%async_computation | async-start | bytes 2359296 | tf_op jit(solution)/shard_map/all_to_all | solution.py:127
  47.7 3.7 %copy-start = (bf16[128,6,512]{0,2,1:T(8,128)(2,1)S(1)}, bf16[128,6,512]{0,2,1:T(8,128)(2,1)}, u32[]{:S(2)}) copy-start(bf16[128,6,512]{0,2,1:T(8,128)(2,1)} %slice.95) | copy-start | bytes 2359300
  56.5 0.9 %copy-start.2 = (bf16[128,1,512]{2,0,1:T(8,128)(2,1)S(1)}, bf16[128,1,512]{2,0,1:T(8,128)(2,1)}, u32[]{:S(2)}) copy-start(bf16[128,1,512]{2,0,1:T(8,128)(2,1)} %copy.40) | copy-start | bytes 393220
  56.5 1.0 %copy-start.3 = (bf16[128,1,512]{2,0,1:T(8,128)(2,1)S(1)}, bf16[128,1,512]{2,0,1:T(8,128)(2,1)}, u32[]{:S(2)}) copy-start(bf16[128,1,512]{2,0,1:T(8,128)(2,1)} %copy.39) | copy-start | bytes 393220
  56.5 1.0 %copy-start.4 = (bf16[128,1,512]{2,0,1:T(8,128)(2,1)S(1)}, bf16[128,1,512]{2,0,1:T(8,128)(2,1)}, u32[]{:S(2)}) copy-start(bf16[128,1,512]{2,0,1:T(8,128)(2,1)} %copy.38) | copy-start | bytes 393220

commit v3 on v1

v3 whole, which is shorter than its diff:
```python
import jax
import jax.numpy as jnp
from jax import lax
from jax.experimental import pallas as pl
from jax.experimental.pallas import tpu as pltpu
from jax.sharding import PartitionSpec as P


LABEL_WIDTH = 128


def buckets(rows, target, local, capacity, number):
    hits = (target[:, None] == jnp.arange(number, dtype=jnp.int32)[None, :]).astype(jnp.int32)
    rank = jnp.sum(hits * (jnp.cumsum(hits, axis=0) - 1), axis=1)
    place = jnp.where(target >= 0, target * capacity + rank, -1)
    picker = (place[:, None] == jnp.arange(number * capacity, dtype=jnp.int32)[None, :]).astype(
        jnp.bfloat16
    )
    packed = jnp.dot(picker.T, rows, preferred_element_type=jnp.float32).astype(jnp.bfloat16)
    labels = (
        jnp.sum(picker.T.astype(jnp.float32) * (local + 1).astype(jnp.float32)[None, :], axis=1)
        - 1.0
    )
    width = rows.shape[1]
    return (
        packed.reshape(number, capacity * width),
        labels.reshape(number, capacity),
    )


def settle(received, labels, streams):
    picker = (labels[:, None] == jnp.arange(streams, dtype=jnp.float32)[None, :]).astype(
        jnp.bfloat16
    )
    return jnp.dot(picker.T, received, preferred_element_type=jnp.float32)


def conv_kernel(own_ref, pan_ref, uw_ref, w_ref, b_ref, lim_ref, o_ref, nc_ref, ext_ref):
    taps = w_ref.shape[0]
    steps, streams, block = o_ref.shape
    rows, _, channels = ext_ref.shape
    kept_rows = own_ref.shape[1] // channels
    frames = pan_ref.shape[1] // channels
    lim = lim_ref[...]

    @pl.when(pl.program_id(0) == 0)
    def _():
        prev = [own_ref[:, 0:channels]] + [
            pan_ref[:, f * channels : (f + 1) * channels] for f in range(frames)
        ]
        for row in range(kept_rows - 1):
            ext_ref[row] = own_ref[:, (row + 1) * channels : (row + 2) * channels]
        weight = uw_ref[...]
        for f in range(frames):
            current = prev[f + 1].astype(jnp.float32)
            earlier = prev[f].astype(jnp.float32)
            for j in range(2):
                value = weight[j : j + 1] * current + weight[j + 2 : j + 3] * earlier
                ext_ref[kept_rows - 1 + 2 * f + j] = value.astype(ext_ref.dtype)
        first = prev[1]
        tail = [ext_ref[2 + i] for i in range(kept_rows - 1)]
        for valid in range(2, frames + 1):
            chosen = lim == 2 * valid
            first = jnp.where(chosen, prev[valid], first)
            tail = [
                jnp.where(chosen, ext_ref[2 * valid + i], tail[i]) for i in range(kept_rows - 1)
            ]
        nc_ref[:, 0:channels] = first
        for i in range(kept_rows - 1):
            nc_ref[:, (i + 1) * channels : (i + 2) * channels] = tail[i]

    acc = None
    for tap in range(taps):
        window = ext_ref[tap : tap + steps].reshape(steps * streams, channels)
        part = jnp.dot(window, w_ref[tap], preferred_element_type=jnp.float32)
        acc = part if acc is None else acc + part
    acc = acc + b_ref[...]
    act = jnp.where(acc > 0, acc, jnp.exp(jnp.minimum(acc, 0.0)) - 1.0)
    act = act.reshape(steps, streams, block)
    for step in range(steps):
        o_ref[step] = jnp.where(step < lim, act[step], 0.0).astype(o_ref.dtype)


def conv_call(owned, panels, up_weight, conv_weight, conv_bias, limit, steps):
    streams, cache_width = owned.shape
    panel_width = panels.shape[1]
    taps, channels, outward = conv_weight.shape
    rows = cache_width // channels - 1 + steps
    block = 256 if outward % 256 == 0 else outward
    whole = lambda n: (0, 0)
    return pl.pallas_call(
        conv_kernel,
        out_shape=(
            jax.ShapeDtypeStruct((steps, streams, outward), jnp.bfloat16),
            jax.ShapeDtypeStruct((streams, cache_width), jnp.bfloat16),
        ),
        grid=(outward // block,),
        in_specs=[
            pl.BlockSpec((streams, cache_width), whole),
            pl.BlockSpec((streams, panel_width), whole),
            pl.BlockSpec(up_weight.shape, whole),
            pl.BlockSpec((taps, channels, block), lambda n: (0, 0, n)),
            pl.BlockSpec((1, block), lambda n: (0, n)),
            pl.BlockSpec((streams, 1), whole),
        ],
        out_specs=(
            pl.BlockSpec((steps, streams, block), lambda n: (0, 0, n)),
            pl.BlockSpec((streams, cache_width), whole),
        ),
        scratch_shapes=[pltpu.VMEM((rows, streams, channels), jnp.bfloat16)],
        compiler_params=pltpu.CompilerParams(dimension_semantics=("arbitrary",)),
    )(owned, panels, up_weight, conv_weight, conv_bias.reshape(1, outward), limit)


def body(latents, cache, panel_slot, cache_slot, frames_valid, up_weight, conv_weight, conv_bias):
    number = lax.axis_size("dec")
    myself = lax.axis_index("dec")
    streams = latents.shape[0]
    frames = latents.shape[1]
    channels = latents.shape[2]
    rows_kept = cache.shape[1]
    pair_cap = max(2, (streams + number - 2) // (number - 1))
    mig_cap = max(2, (streams // 2 + number - 3) // (number - 2))
    panel_width = frames * channels
    cache_width = rows_kept * channels
    flat_latents = latents.reshape(streams, panel_width)
    flat_cache = cache.reshape(streams, cache_width)
    panel_owner = panel_slot // streams
    panel_local = panel_slot % streams
    cache_owner = cache_slot // streams
    cache_local = cache_slot % streams
    moving = cache_owner != myself
    staying = jnp.logical_not(moving)
    stay_pick = (
        staying[:, None] & (cache_local[:, None] == jnp.arange(streams, dtype=jnp.int32)[None, :])
    ).astype(jnp.bfloat16)
    kept = jnp.dot(stay_pick.T, flat_cache, preferred_element_type=jnp.float32)
    cache_send, cache_labels = buckets(
        flat_cache, jnp.where(moving, cache_owner, -1), cache_local, mig_cap, number
    )
    panel_send, panel_labels = buckets(flat_latents, panel_owner, panel_local, pair_cap, number)
    lane = LABEL_WIDTH
    panel_rows = pair_cap * panel_width // lane
    cache_rows = mig_cap * cache_width // lane
    label_rows = -(panel_rows + cache_rows + 1) % 16 + 1
    label_block = jnp.concatenate([panel_labels, cache_labels], axis=1)
    label_block = jnp.pad(
        label_block, ((0, 0), (0, label_rows * lane - label_block.shape[1])), constant_values=-1.0
    ).astype(jnp.bfloat16)
    joint = jnp.concatenate(
        [
            panel_send.reshape(number, panel_rows, lane),
            cache_send.reshape(number, cache_rows, lane),
            label_block.reshape(number, label_rows, lane),
        ],
        axis=1,
    )
    joint_recv = lax.all_to_all(joint, "dec", split_axis=0, concat_axis=0, tiled=True)
    panel_recv = joint_recv[:, :panel_rows].reshape(number * pair_cap, panel_width)
    cache_recv = joint_recv[:, panel_rows : panel_rows + cache_rows].reshape(
        number * mig_cap, cache_width
    )
    recv_labels = joint_recv[:, panel_rows + cache_rows, :].astype(jnp.float32)
    panel_rl = recv_labels[:, :pair_cap].reshape(-1)
    cache_rl = recv_labels[:, pair_cap : pair_cap + mig_cap].reshape(-1)
    panels = settle(panel_recv, panel_rl, streams).astype(jnp.bfloat16)
    arrived = settle(cache_recv, cache_rl, streams)
    owned = (kept + arrived).astype(jnp.bfloat16)
    limit = (2 * frames_valid).reshape(streams, 1)
    decoded_t, new_cache = conv_call(
        owned, panels, up_weight, conv_weight, conv_bias, limit, 2 * frames
    )
    decoded = jnp.transpose(decoded_t, (1, 0, 2))
    new_cache = new_cache.reshape(streams, rows_kept, channels)
    return (decoded, new_cache)


def solution(mesh):
    in_specs = (
        P(("grp", "dec"), None, None),
        P(("grp", "dec"), None, None),
        P(("grp", "dec")),
        P(("grp", "dec")),
        P(("grp", "dec")),
        P(),
        P(),
        P(),
    )
    out_specs = (P(("grp", "dec"), None, None), P(("grp", "dec"), None, None))
    return jax.shard_map(body, mesh=mesh, in_specs=in_specs, out_specs=out_specs, check_vma=False)
```

time: 85.7 us -> 66 us (0.77)
  local copies, waits for them, and re-layouts: 27.1 us -> 11 us
  other arithmetic: 9.65 us -> 4.3 us
  matrix products: 2.4 us -> 4.11 us
    unnamed x25 -> x10, local copies, waits for them, and re-layouts: 17.2 us -> 7.2 us
    slice x8 -> x2, local copies, waits for them, and re-layouts: 3.88 us -> 0.08 us  [the longest x1 0.04 us: body(): joint_recv[:, panel_rows:panel_rows + cache_rows]]
    reshape x4 -> x3, local copies, waits for them, and re-layouts: 2.89 us -> 0.9 us  [the longest x1 0.64 us: body(): joint_recv[:, panel_rows:panel_rows + cache_rows]]
    another operation x5 -> x2, other arithmetic: 1.76 us -> 0.01 us  [the longest x3 1.75 us: body(): jnp.stack([even, odd], axis=1).reshape(2 * frames, streams, channels)]
    all_to_all x2 -> x0, other arithmetic: 1.61 us -> none  [body(): lax.all_to_all(joint, 'dec', split_axis=0, concat_axis=0, tiled=True)]
    concatenate x2 -> x1, other arithmetic: 2.39 us -> 1.1 us  [body(): jnp.concatenate([panel_send.reshape(number, panel_rows, lane), cache_send...]
    dot_general x1, matrix products: 0.53 us -> 1.44 us  [body(): kept = jnp.dot(stay_pick.T, flat_cache, preferred_element_type=jnp.float32)]
    convert_element_type x2 -> x0, local copies, waits for them, and re-layouts: 0.89 us -> none  [the longest x1 0.62 us: body(): (kept + arrived).astype(jnp.bfloat16).reshape(streams, rows_kept, channels)]
where the time goes in v3:
time: 66 us; the launch traced here: 65.8 us
  waiting for transfers between devices  27 us (41%)
  Pallas kernels  12 us (18%)
  local copies, waits for them, and re-layouts  11 us (17%)
  starting transfers between devices  6.56 us (10%)
  other arithmetic  4.3 us (7%)
  matrix products  4.11 us (6%)
  between operations  0.84 us (1%)
    all_to_all x1, waiting for transfers between devices, body(): lax.all_to_all(joint, 'dec', split_axis=0, concat_axis=0, tiled=True)  27 us
    pallas_call x1, Pallas kernels, conv_call(): pl.pallas_call(conv_kernel, out_shape=(jax.ShapeDtypeStruct((steps, strea...  12 us
    unnamed x10, local copies, waits for them, and re-layouts  7.2 us
    all_to_all x1, starting transfers between devices, body(): lax.all_to_all(joint, 'dec', split_axis=0, concat_axis=0, tiled=True)  6.56 us
    dot_general x2, matrix products, settle(): return jnp.dot(picker.T, received, preferred_element_type=jnp.float32)  1.72 us
    dot_general x1, matrix products, body(): kept = jnp.dot(stay_pick.T, flat_cache, preferred_element_type=jnp.float32)  1.44 us
  transfers between devices with their start and end apart: 1, of which 1 were waited for; matrix products, arithmetic and copies ran while one was open for 1% of the time, Pallas kernels for 0%

profile of v3, /device:TPU:13, one launch (start us, length us, event | category | flops | bytes accessed | tf_op | source)
XLA Modules:
  0.0 65.8 jit_solution(8664951642619000417)
XLA Ops:
  0.6 0.7 %and_select_fusion.1 = (s32[128]{0:T(128)S(1)}, f32[128]{0:T(128)S(1)}) fusion(s32[128]{0:T(128)} %param.10), kind=kLoop, calls=%fused_computation.43 | loop fusion | flops 2688 | bytes 1536 | tf_op jit(solution)/shard_map/jit(floor_divide)/jit(_where)/select_n | solution.py:128
  1.3 0.7 %compare_not_fusion = (pred[128]{0:T(512)(128)(4,1)S(1)}, s32[128]{0:T(128)S(1)}) fusion(s32[]{:T(128)S(6)} %axis_index.12, s32[128]{0:T(128)} %param.11), kind=kLoop, calls=%fused_computation.39 | loop fusion | flops 2176 | bytes 1156 | tf_op jit(solution)/shard_map/not | solution.py:133
  2.0 0.1 fusion.2
  2.1 0.2 reduce_window_sum.18
  2.2 0.2 select_reduce_fusion
  2.4 0.7 %add_convert_fusion.2 = (f32[128]{0:T(128)S(1)}, s32[128]{0:T(128)S(1)}, s32[128]{0:T(128)S(1)}) fusion(s32[128]{0:T(128)} %param.11, s32[128]{0:T(128)S(1)} %select_reduce_fusion, s32[128]{0:T(128)S(1)} %get-tuple-element.13, s32[]{:T(128)S(6)} %axis_index.12), kind=kLoop, calls=%fused_computation.57 | loop fusion | flops 2432 | bytes 3076 | tf_op jit(solution)/shard_map/convert_element_type | solution.py:21
  3.1 0.1 multiply_reduce_fusion.1
  3.2 0.1 sub.35
  3.3 0.0 copy-start
  3.3 0.1 fusion.4
  3.4 0.2 reduce_window_sum.17
  3.6 0.2 select_reduce_fusion.1
  3.8 0.1 multiply_reduce_fusion
  3.9 0.1 sub.33
  4.0 0.1 fusion.19
  4.1 1.1 %copy.25 = bf16[16,8,4,512]{3,1,2,0:T(8,128)(2,1)S(1)} copy(bf16[16,8,4,512]{3,2,1,0:T(4,128)(2,1)} %bitcast.20) | data formatting | bytes 1048576
  5.3 0.4 convolution_convert_fusion.1
  5.7 0.3 reshape_reshape.6
  6.0 0.0 copy-done
  6.0 0.6 copy.20
  6.6 0.5 convolution_convert_fusion
  7.1 0.7 %reshape_reshape.7 = bf16[16,140,128]{2,1,0:T(8,128)(2,1)S(1)} reshape(bf16[80,3584]{1,0:T(8,128)(2,1)S(1)} %convolution_convert_fusion) | data formatting | bytes 1146880 | tf_op jit(solution)/shard_map/reshape;reshape | solution.py:153
  7.9 0.0 copy-start.2
  7.9 1.1 %pad_maximum_fusion = bf16[16,288,128]{2,1,0:T(8,128)(2,1)} fusion(bf16[16,4,128]{2,1,0:T(4,128)(2,1)S(1)} %reshape.52, bf16[16,140,128]{2,1,0:T(8,128)(2,1)S(1)} %reshape_reshape.7, bf16[16,144,128]{2,1,0:T(8,128)(2,1)S(1)} %reshape_reshape.6), kind=kLoop, calls=%fused_computation.5 | loop fusion | flops 3538944 | bytes 2359296 | tf_op jit(solution)/shard_map/concatenate | solution.py:150
  9.0 6.6 %all-to-all-start = ((bf16[16,288,128]{2,1,0:T(8,128)(2,1)}), bf16[16,288,128]{2,1,0:T(8,128)(2,1)S(1)}, u32[]{:S(2)}, u32[]{:S(2)}) async-start(bf16[16,288,128]{2,1,0:T(8,128)(2,1)} %pad_maximum_fusion), calls=%async_computation | async-start | bytes 2359296 | tf_op jit(solution)/shard_map/all_to_all | solution.py:158
  15.6 0.0 copy-done.2
  15.6 0.7 %copy.21.lim_ref = s32[128,1]{1,0:T(8,128)} copy(s32[128,1]{0,1:T(1,128)S(1)} %multiply_bitcast_fusion) | data formatting | bytes 1024 | tf_op jit(solution)/shard_map/reshape | solution.py:169
  16.3 27.0 %all-to-all-done = bf16[16,288,128]{2,1,0:T(8,128)(2,1)S(1)} async-done(((bf16[16,288,128]{2,1,0:T(8,128)(2,1)}), bf16[16,288,128]{2,1,0:T(8,128)(2,1)S(1)}, u32[]{:S(2)}, u32[]{:S(2)}) %all-to-all-start) | async-done | bytes 1179680 | tf_op jit(solution)/shard_map/all_to_all | solution.py:158
  43.3 0.1 slice.21
  43.4 0.1 eq.137
  43.5 0.1 eq.133
  43.6 0.6 reshape.53
  44.3 0.3 reshape.54
  44.6 1.2 %convolution_convert_fusion.2.pan_ref = bf16[128,2048]{1,0:T(8,128)(2,1)} fusion(bf16[144,2048]{1,0:T(8,128)(2,1)S(1)} %reshape.54, f32[144]{0:T(256)S(1)} %eq.137), kind=kOutput, calls=%fused_computation.4 | convolution fusion | flops 75778048 | bytes 1114688 | tf_op jit(solution)/shard_map/dot_general | solution.py:35
  45.8 0.5 fusion.9
  46.3 1.4 %fusion.own_ref = bf16[128,3584]{1,0:T(8,128)(2,1)} fusion(f32[128,3584]{1,0:T(8,128)S(1)} %fusion.9, bf16[128,3584]{0,1:T(8,128)(2,1)S(1)} %bitcast.16, s32[128]{0:T(128)S(1)} %get-tuple-element.15, pred[128]{0:T(512)(128)(4,1)S(1)} %get-tuple-element.12), kind=kOutput, calls=%fused_computation.1 | convolution fusion | flops 118407168 | bytes 3670656 | tf_op jit(solution)/shard_map/dot_general | solution.py:137
  47.7 12.0 %shard_map.95 = (bf16[8,128,1024]{2,1,0:T(8,128)(2,1)}, bf16[128,3584]{1,0:T(8,128)(2,1)}) custom-call(bf16[128,3584]{1,0:T(8,128)(2,1)} %fusion.own_ref, bf16[128,2048]{1,0:T(8,128)(2,1)} %convolution_convert_fusion.2.pan_ref, f32[4,512]{1,0:T(4,128)} %uw_ref.1, bf16[7,512,1024]{2,1,0:T(8,128)(2,1)} %w_ref.1, f32[1,1024]{1,0:T(1,128)} %bitcast.23, ...), custom_call_target="tpu_custom_call" | custom-call | tf_op jit(solution)/shard_map/pallas_call | solution.py:91
  59.7 0.0 copy-start.1
  59.7 4.1 %copy.23 = bf16[128,8,1024]{2,1,0:T(8,128)(2,1)} copy(bf16[128,8,1024]{2,0,1:T(8,128)(2,1)} %bitcast.18) | data formatting | bytes 4194304
  63.9 0.0 copy-done.1
  63.9 0.6 copy.22
  64.5 1.3 %copy.24 = bf16[128,7,512]{2,0,1:T(8,128)(2,1)} copy(bf16[128,7,512]{0,2,1:T(8,128)(2,1)S(1)} %bitcast.17) | data formatting | bytes 1835008
  (9 shorter events, 0.1 us)
Async XLA Ops:
  3.3 2.6 %copy-start = (bf16[128,7,512]{2,0,1:T(8,128)(2,1)S(1)}, bf16[128,7,512]{2,0,1:T(8,128)(2,1)}, u32[]{:S(2)}) copy-start(bf16[128,7,512]{2,0,1:T(8,128)(2,1)} %param.9) | copy-start | bytes 2752516
  7.9 7.7 %copy-start.2 = (s32[128]{0:T(128)S(1)}, s32[128]{0:T(128)}, u32[]{:S(2)}) copy-start(s32[128]{0:T(128)} %param.12) | copy-start | bytes 1540
  9.0 34.3 %all-to-all-start = ((bf16[16,288,128]{2,1,0:T(8,128)(2,1)}), bf16[16,288,128]{2,1,0:T(8,128)(2,1)S(1)}, u32[]{:S(2)}, u32[]{:S(2)}) async-start(bf16[16,288,128]{2,1,0:T(8,128)(2,1)} %pad_maximum_fusion), calls=%async_computation | async-start | bytes 2359296 | tf_op jit(solution)/shard_map/all_to_all | solution.py:158
  59.7 4.1 %copy-start.1 = (bf16[128,3584]{1,0:T(8,128)(2,1)S(1)}, bf16[128,3584]{1,0:T(8,128)(2,1)}, u32[]{:S(2)}) copy-start(bf16[128,3584]{1,0:T(8,128)(2,1)} %get-tuple-element.5) | copy-start | bytes 2752516

commit v4 on v3

--- a/solution.py
+++ b/solution.py
@@ -37,7 +37,7 @@
 
 def conv_kernel(own_ref, pan_ref, uw_ref, w_ref, b_ref, lim_ref, o_ref, nc_ref, ext_ref):
     taps = w_ref.shape[0]
-    steps, streams, block = o_ref.shape
+    streams, steps, block = o_ref.shape
     rows, _, channels = ext_ref.shape
     kept_rows = own_ref.shape[1] // channels
     frames = pan_ref.shape[1] // channels
@@ -65,9 +65,9 @@
             tail = [
                 jnp.where(chosen, ext_ref[2 * valid + i], tail[i]) for i in range(kept_rows - 1)
             ]
-        nc_ref[:, 0:channels] = first
+        nc_ref[0] = first
         for i in range(kept_rows - 1):
-            nc_ref[:, (i + 1) * channels : (i + 2) * channels] = tail[i]
+            nc_ref[i + 1] = tail[i]
 
     acc = None
     for tap in range(taps):
@@ -78,7 +78,7 @@
     act = jnp.where(acc > 0, acc, jnp.exp(jnp.minimum(acc, 0.0)) - 1.0)
     act = act.reshape(steps, streams, block)
     for step in range(steps):
-        o_ref[step] = jnp.where(step < lim, act[step], 0.0).astype(o_ref.dtype)
+        o_ref[:, step, :] = jnp.where(step < lim, act[step], 0.0).astype(o_ref.dtype)
 
 
 def conv_call(owned, panels, up_weight, conv_weight, conv_bias, limit, steps):
@@ -91,8 +91,8 @@
     return pl.pallas_call(
         conv_kernel,
         out_shape=(
-            jax.ShapeDtypeStruct((steps, streams, outward), jnp.bfloat16),
-            jax.ShapeDtypeStruct((streams, cache_width), jnp.bfloat16),
+            jax.ShapeDtypeStruct((streams, steps, outward), jnp.bfloat16),
+            jax.ShapeDtypeStruct((cache_width // channels, streams, channels), jnp.bfloat16),
         ),
         grid=(outward // block,),
         in_specs=[
@@ -104,8 +104,8 @@
             pl.BlockSpec((streams, 1), whole),
         ],
         out_specs=(
-            pl.BlockSpec((steps, streams, block), lambda n: (0, 0, n)),
-            pl.BlockSpec((streams, cache_width), whole),
+            pl.BlockSpec((streams, steps, block), lambda n: (0, 0, n)),
+            pl.BlockSpec((cache_width // channels, streams, channels), lambda n: (0, 0, 0)),
         ),
         scratch_shapes=[pltpu.VMEM((rows, streams, channels), jnp.bfloat16)],
         compiler_params=pltpu.CompilerParams(dimension_semantics=("arbitrary",)),
@@ -167,11 +167,10 @@
     arrived = settle(cache_recv, cache_rl, streams)
     owned = (kept + arrived).astype(jnp.bfloat16)
     limit = (2 * frames_valid).reshape(streams, 1)
-    decoded_t, new_cache = conv_call(
+    decoded, new_cache = conv_call(
         owned, panels, up_weight, conv_weight, conv_bias, limit, 2 * frames
     )
-    decoded = jnp.transpose(decoded_t, (1, 0, 2))
-    new_cache = new_cache.reshape(streams, rows_kept, channels)
+    new_cache = jnp.transpose(new_cache, (1, 0, 2))
     return (decoded, new_cache)
 
 

time: 66 us -> 62.4 us (0.945)
  local copies, waits for them, and re-layouts: 11 us -> 4.94 us
  Pallas kernels: 12 us -> 14.4 us
    unnamed x10 -> x6, local copies, waits for them, and re-layouts: 7.2 us -> 1.78 us
    pallas_call x1, Pallas kernels: 12 us -> 14.4 us  [conv_call(): pl.pallas_call(conv_kernel, out_shape=(jax.ShapeDtypeStruct((streams, ste...]
where the time goes in v4:
time: 62.4 us; the launch traced here: 62.2 us
  waiting for transfers between devices  27 us (43%)
  Pallas kernels  14.4 us (23%)
  starting transfers between devices  6.56 us (11%)
  local copies, waits for them, and re-layouts  4.94 us (8%)
  other arithmetic  4.3 us (7%)
  matrix products  4.11 us (7%)
  between operations  0.83 us (1%)
    all_to_all x1, waiting for transfers between devices, body(): lax.all_to_all(joint, 'dec', split_axis=0, concat_axis=0, tiled=True)  27 us
    pallas_call x1, Pallas kernels, conv_call(): pl.pallas_call(conv_kernel, out_shape=(jax.ShapeDtypeStruct((streams, ste...  14.4 us
    all_to_all x1, starting transfers between devices, body(): lax.all_to_all(joint, 'dec', split_axis=0, concat_axis=0, tiled=True)  6.56 us
    unnamed x6, local copies, waits for them, and re-layouts  1.78 us
    dot_general x2, matrix products, settle(): return jnp.dot(picker.T, received, preferred_element_type=jnp.float32)  1.72 us
    dot_general x1, matrix products, body(): kept = jnp.dot(stay_pick.T, flat_cache, preferred_element_type=jnp.float32)  1.45 us
  transfers between devices with their start and end apart: 1, of which 1 were waited for; matrix products, arithmetic and copies ran while one was open for 1% of the time, Pallas kernels for 0%

profile of v4, /device:TPU:13, one launch (start us, length us, event | category | flops | bytes accessed | tf_op | source)
XLA Modules:
  0.0 62.2 jit_solution(4708386123332678198)
XLA Ops:
  0.6 0.7 %and_select_fusion.1 = (s32[128]{0:T(128)S(1)}, f32[128]{0:T(128)S(1)}) fusion(s32[128]{0:T(128)} %param.10), kind=kLoop, calls=%fused_computation.43 | loop fusion | flops 2688 | bytes 1536 | tf_op jit(solution)/shard_map/jit(floor_divide)/jit(_where)/select_n | solution.py:128
  1.3 0.7 %compare_not_fusion = (pred[128]{0:T(512)(128)(4,1)S(1)}, s32[128]{0:T(128)S(1)}) fusion(s32[]{:T(128)S(6)} %axis_index.12, s32[128]{0:T(128)} %param.11), kind=kLoop, calls=%fused_computation.39 | loop fusion | flops 2176 | bytes 1156 | tf_op jit(solution)/shard_map/not | solution.py:133
  2.0 0.1 fusion.2
  2.1 0.2 reduce_window_sum.18
  2.2 0.2 select_reduce_fusion
  2.4 0.7 %add_convert_fusion.2 = (f32[128]{0:T(128)S(1)}, s32[128]{0:T(128)S(1)}, s32[128]{0:T(128)S(1)}) fusion(s32[128]{0:T(128)} %param.11, s32[128]{0:T(128)S(1)} %select_reduce_fusion, s32[128]{0:T(128)S(1)} %get-tuple-element.7, s32[]{:T(128)S(6)} %axis_index.12), kind=kLoop, calls=%fused_computation.57 | loop fusion | flops 2432 | bytes 3076 | tf_op jit(solution)/shard_map/convert_element_type | solution.py:21
  3.1 0.1 multiply_reduce_fusion.1
  3.2 0.1 sub.35
  3.3 0.0 copy-start
  3.3 0.1 fusion.4
  3.4 0.2 reduce_window_sum.17
  3.6 0.2 select_reduce_fusion.1
  3.8 0.1 multiply_reduce_fusion
  3.9 0.1 sub.33
  4.0 0.1 fusion.19
  4.1 1.1 %copy.17 = bf16[16,8,4,512]{3,1,2,0:T(8,128)(2,1)S(1)} copy(bf16[16,8,4,512]{3,2,1,0:T(4,128)(2,1)} %bitcast.17) | data formatting | bytes 1048576
  5.3 0.4 convolution_convert_fusion.1
  5.7 0.3 reshape_reshape.6
  6.0 0.0 copy-done
  6.0 0.6 copy.15
  6.6 0.5 convolution_convert_fusion
  7.1 0.7 %reshape_reshape.7 = bf16[16,140,128]{2,1,0:T(8,128)(2,1)S(1)} reshape(bf16[80,3584]{1,0:T(8,128)(2,1)S(1)} %convolution_convert_fusion) | data formatting | bytes 1146880 | tf_op jit(solution)/shard_map/reshape;reshape | solution.py:153
  7.9 0.0 copy-start.1
  7.9 1.1 %pad_maximum_fusion = bf16[16,288,128]{2,1,0:T(8,128)(2,1)} fusion(bf16[16,4,128]{2,1,0:T(4,128)(2,1)S(1)} %reshape.49, bf16[16,140,128]{2,1,0:T(8,128)(2,1)S(1)} %reshape_reshape.7, bf16[16,144,128]{2,1,0:T(8,128)(2,1)S(1)} %reshape_reshape.6), kind=kLoop, calls=%fused_computation.5 | loop fusion | flops 3538944 | bytes 2359296 | tf_op jit(solution)/shard_map/concatenate | solution.py:150
  9.0 6.6 %all-to-all-start = ((bf16[16,288,128]{2,1,0:T(8,128)(2,1)}), bf16[16,288,128]{2,1,0:T(8,128)(2,1)S(1)}, u32[]{:S(2)}, u32[]{:S(2)}) async-start(bf16[16,288,128]{2,1,0:T(8,128)(2,1)} %pad_maximum_fusion), calls=%async_computation | async-start | bytes 2359296 | tf_op jit(solution)/shard_map/all_to_all | solution.py:158
  15.6 0.0 copy-done.1
  15.6 0.7 %copy.16.lim_ref = s32[128,1]{1,0:T(8,128)} copy(s32[128,1]{0,1:T(1,128)S(1)} %multiply_bitcast_fusion) | data formatting | bytes 1024 | tf_op jit(solution)/shard_map/reshape | solution.py:169
  16.3 27.0 %all-to-all-done = bf16[16,288,128]{2,1,0:T(8,128)(2,1)S(1)} async-done(((bf16[16,288,128]{2,1,0:T(8,128)(2,1)}), bf16[16,288,128]{2,1,0:T(8,128)(2,1)S(1)}, u32[]{:S(2)}, u32[]{:S(2)}) %all-to-all-start) | async-done | bytes 1179680 | tf_op jit(solution)/shard_map/all_to_all | solution.py:158
  43.3 0.1 slice.21
  43.4 0.1 eq.137
  43.5 0.1 eq.133
  43.6 0.6 %reshape.50 = bf16[80,3584]{1,0:T(8,128)(2,1)S(1)} reshape(bf16[16,140,128]{2,1,0:T(8,128)(2,1)S(1)} %slice.22) | data formatting | bytes 1146880 | tf_op jit(solution)/shard_map/reshape | solution.py:160
  44.3 0.3 reshape.51
  44.6 1.2 %convolution_convert_fusion.2.pan_ref = bf16[128,2048]{1,0:T(8,128)(2,1)} fusion(bf16[144,2048]{1,0:T(8,128)(2,1)S(1)} %reshape.51, f32[144]{0:T(256)S(1)} %eq.137), kind=kOutput, calls=%fused_computation.4 | convolution fusion | flops 75778048 | bytes 1114688 | tf_op jit(solution)/shard_map/dot_general | solution.py:35
  45.8 0.5 fusion.9
  46.3 1.4 %fusion.own_ref = bf16[128,3584]{1,0:T(8,128)(2,1)} fusion(f32[128,3584]{1,0:T(8,128)S(1)} %fusion.9, bf16[128,3584]{0,1:T(8,128)(2,1)S(1)} %bitcast.15, s32[128]{0:T(128)S(1)} %get-tuple-element.9, pred[128]{0:T(512)(128)(4,1)S(1)} %get-tuple-element.6), kind=kOutput, calls=%fused_computation.1 | convolution fusion | flops 118407168 | bytes 3670656 | tf_op jit(solution)/shard_map/dot_general | solution.py:137
  47.7 14.4 %shard_map.95 = (bf16[128,8,1024]{2,1,0:T(8,128)(2,1)}, bf16[7,128,512]{2,1,0:T(8,128)(2,1)}) custom-call(bf16[128,3584]{1,0:T(8,128)(2,1)} %fusion.own_ref, bf16[128,2048]{1,0:T(8,128)(2,1)} %convolution_convert_fusion.2.pan_ref, f32[4,512]{1,0:T(4,128)} %uw_ref.1, bf16[7,512,1024]{2,1,0:T(8,128)(2,1)} %w_ref.1, f32[1,1024]{1,0:T(1,128)} %bitcast.20, ...), custom_call_target="tpu_custom_call" | custom-call | tf_op jit(solution)/shard_map/pallas_call | solution.py:91
  (9 shorter events, 0.1 us)
Async XLA Ops:
  3.3 2.6 %copy-start = (bf16[128,7,512]{2,0,1:T(8,128)(2,1)S(1)}, bf16[128,7,512]{2,0,1:T(8,128)(2,1)}, u32[]{:S(2)}) copy-start(bf16[128,7,512]{2,0,1:T(8,128)(2,1)} %param.9) | copy-start | bytes 2752516
  7.9 7.7 %copy-start.1 = (s32[128]{0:T(128)S(1)}, s32[128]{0:T(128)}, u32[]{:S(2)}) copy-start(s32[128]{0:T(128)} %param.12) | copy-start | bytes 1540
  9.0 34.3 %all-to-all-start = ((bf16[16,288,128]{2,1,0:T(8,128)(2,1)}), bf16[16,288,128]{2,1,0:T(8,128)(2,1)S(1)}, u32[]{:S(2)}, u32[]{:S(2)}) async-start(bf16[16,288,128]{2,1,0:T(8,128)(2,1)} %pad_maximum_fusion), calls=%async_computation | async-start | bytes 2359296 | tf_op jit(solution)/shard_map/all_to_all | solution.py:158

commit v5 on v4

--- a/solution.py
+++ b/solution.py
@@ -28,28 +28,47 @@
     )
 
 
-def settle(received, labels, streams):
-    picker = (labels[:, None] == jnp.arange(streams, dtype=jnp.float32)[None, :]).astype(
-        jnp.bfloat16
-    )
-    return jnp.dot(picker.T, received, preferred_element_type=jnp.float32)
-
-
-def conv_kernel(own_ref, pan_ref, uw_ref, w_ref, b_ref, lim_ref, o_ref, nc_ref, ext_ref):
+def pick(labels, streams):
+    target = lax.broadcasted_iota(jnp.int32, (streams, labels.shape[1]), 0).astype(jnp.float32)
+    return (target == labels).astype(jnp.bfloat16)
+
+
+def conv_kernel(
+    cache_ref, crecv_ref, precv_ref, klab_ref, clab_ref, plab_ref, uw_ref, w_ref, b_ref,
+    lim_ref, o_ref, nc_ref, ext_ref,
+):
     taps = w_ref.shape[0]
     streams, steps, block = o_ref.shape
     rows, _, channels = ext_ref.shape
-    kept_rows = own_ref.shape[1] // channels
-    frames = pan_ref.shape[1] // channels
+    kept_rows = cache_ref.shape[0]
+    frames = precv_ref.shape[1] // channels
     lim = lim_ref[...]
 
     @pl.when(pl.program_id(0) == 0)
     def _():
-        prev = [own_ref[:, 0:channels]] + [
-            pan_ref[:, f * channels : (f + 1) * channels] for f in range(frames)
+        keep_pick = pick(klab_ref[...], streams)
+        cache_pick = pick(clab_ref[...], streams)
+        panel_pick = pick(plab_ref[...], streams)
+
+        def owned(row):
+            here = jnp.dot(keep_pick, cache_ref[row], preferred_element_type=jnp.float32)
+            came = jnp.dot(
+                cache_pick,
+                crecv_ref[:, row * channels : (row + 1) * channels],
+                preferred_element_type=jnp.float32,
+            )
+            return (here + came).astype(ext_ref.dtype)
+
+        prev = [owned(0)] + [
+            jnp.dot(
+                panel_pick,
+                precv_ref[:, f * channels : (f + 1) * channels],
+                preferred_element_type=jnp.float32,
+            ).astype(ext_ref.dtype)
+            for f in range(frames)
         ]
         for row in range(kept_rows - 1):
-            ext_ref[row] = own_ref[:, (row + 1) * channels : (row + 2) * channels]
+            ext_ref[row] = owned(row + 1)
         weight = uw_ref[...]
         for f in range(frames):
             current = prev[f + 1].astype(jnp.float32)
@@ -81,35 +100,43 @@
         o_ref[:, step, :] = jnp.where(step < lim, act[step], 0.0).astype(o_ref.dtype)
 
 
-def conv_call(owned, panels, up_weight, conv_weight, conv_bias, limit, steps):
-    streams, cache_width = owned.shape
-    panel_width = panels.shape[1]
-    taps, channels, outward = conv_weight.shape
-    rows = cache_width // channels - 1 + steps
+def conv_call(cache_t, crecv, precv, klab, clab, plab, up_weight, conv_weight, conv_bias, limit, steps):
+    kept_rows, streams, channels = cache_t.shape
+    taps, _, outward = conv_weight.shape
+    rows = kept_rows - 1 + steps
     block = 256 if outward % 256 == 0 else outward
     whole = lambda n: (0, 0)
+    operands = (cache_t, crecv, precv, klab, clab, plab, up_weight)
+    in_specs = [pl.BlockSpec(cache_t.shape, lambda n: (0, 0, 0))] + [
+        pl.BlockSpec(x.shape, whole) for x in operands[1:]
+    ]
     return pl.pallas_call(
         conv_kernel,
         out_shape=(
             jax.ShapeDtypeStruct((streams, steps, outward), jnp.bfloat16),
-            jax.ShapeDtypeStruct((cache_width // channels, streams, channels), jnp.bfloat16),
+            jax.ShapeDtypeStruct(cache_t.shape, jnp.bfloat16),
         ),
         grid=(outward // block,),
-        in_specs=[
-            pl.BlockSpec((streams, cache_width), whole),
-            pl.BlockSpec((streams, panel_width), whole),
-            pl.BlockSpec(up_weight.shape, whole),
+        in_specs=in_specs
+        + [
             pl.BlockSpec((taps, channels, block), lambda n: (0, 0, n)),
             pl.BlockSpec((1, block), lambda n: (0, n)),
             pl.BlockSpec((streams, 1), whole),
         ],
         out_specs=(
             pl.BlockSpec((streams, steps, block), lambda n: (0, 0, n)),
-            pl.BlockSpec((cache_width // channels, streams, channels), lambda n: (0, 0, 0)),
+            pl.BlockSpec(cache_t.shape, lambda n: (0, 0, 0)),
         ),
         scratch_shapes=[pltpu.VMEM((rows, streams, channels), jnp.bfloat16)],
         compiler_params=pltpu.CompilerParams(dimension_semantics=("arbitrary",)),
-    )(owned, panels, up_weight, conv_weight, conv_bias.reshape(1, outward), limit)
+    )(*operands, conv_weight, conv_bias.reshape(1, outward), limit)
+
+
+def padded(rows, labels):
+    extra = -rows.shape[0] % 128
+    rows = jnp.pad(rows, ((0, extra), (0, 0)))
+    labels = jnp.pad(labels, (0, extra), constant_values=-1.0)
+    return rows, labels.reshape(1, -1)
 
 
 def body(latents, cache, panel_slot, cache_slot, frames_valid, up_weight, conv_weight, conv_bias):
@@ -131,10 +158,7 @@
     cache_local = cache_slot % streams
     moving = cache_owner != myself
     staying = jnp.logical_not(moving)
-    stay_pick = (
-        staying[:, None] & (cache_local[:, None] == jnp.arange(streams, dtype=jnp.int32)[None, :])
-    ).astype(jnp.bfloat16)
-    kept = jnp.dot(stay_pick.T, flat_cache, preferred_element_type=jnp.float32)
+    keep_labels = jnp.where(staying, cache_local, -1).astype(jnp.float32).reshape(1, streams)
     cache_send, cache_labels = buckets(
         flat_cache, jnp.where(moving, cache_owner, -1), cache_local, mig_cap, number
     )
@@ -163,12 +187,13 @@
     recv_labels = joint_recv[:, panel_rows + cache_rows, :].astype(jnp.float32)
     panel_rl = recv_labels[:, :pair_cap].reshape(-1)
     cache_rl = recv_labels[:, pair_cap : pair_cap + mig_cap].reshape(-1)
-    panels = settle(panel_recv, panel_rl, streams).astype(jnp.bfloat16)
-    arrived = settle(cache_recv, cache_rl, streams)
-    owned = (kept + arrived).astype(jnp.bfloat16)
+    precv, plab = padded(panel_recv, panel_rl)
+    crecv, clab = padded(cache_recv, cache_rl)
     limit = (2 * frames_valid).reshape(streams, 1)
+    cache_t = jnp.transpose(cache, (1, 0, 2))
     decoded, new_cache = conv_call(
-        owned, panels, up_weight, conv_weight, conv_bias, limit, 2 * frames
+        cache_t, crecv, precv, keep_labels, clab, plab, up_weight, conv_weight, conv_bias,
+        limit, 2 * frames,
     )
     new_cache = jnp.transpose(new_cache, (1, 0, 2))
     return (decoded, new_cache)

time: 62.4 us -> 64 us (1.026)
  local copies, waits for them, and re-layouts: 4.94 us -> 8.69 us
  matrix products: 4.11 us -> 0.95 us
  Pallas kernels: 14.4 us -> 15.4 us
    dot_general x3 -> x0, matrix products: 3.17 us -> none  [the longest x2 1.72 us: settle(): return jnp.dot(picker.T, received, preferred_element_type=jnp.float32)]
    pad x0 -> x3, local copies, waits for them, and re-layouts: none -> 2.7 us  [the longest x2 2.13 us: padded(): rows = jnp.pad(rows, ((0, extra), (0, 0)))]
    reshape x0 -> x1, other arithmetic: none -> 1.15 us  [body(): jnp.where(staying, cache_local, -1).astype(jnp.float32).reshape(1, streams)]
    pallas_call x1, Pallas kernels: 14.4 us -> 15.4 us  [conv_call(): pl.pallas_call(conv_kernel, out_shape=(jax.ShapeDtypeStruct((streams, ste...]
    reshape x0 -> x3, local copies, waits for them, and re-layouts: none -> 0.77 us  [the longest x1 0.6 us: padded(): return (rows, labels.reshape(1, -1))]
    convert_element_type x1 -> x0, other arithmetic: 0.68 us -> none  [buckets(): (local + 1).astype(jnp.float32)[None, :]]
    not x1 -> x0, other arithmetic: 0.67 us -> none  [body(): staying = jnp.logical_not(moving)]
where the time goes in v5:
time: 64 us; the launch traced here: 63.7 us
  waiting for transfers between devices  27 us (42%)
  Pallas kernels  15.4 us (24%)
  local copies, waits for them, and re-layouts  8.69 us (14%)
  starting transfers between devices  6.69 us (10%)
  other arithmetic  4.13 us (6%)
  matrix products  0.95 us (1%)
  between operations  0.81 us (1%)
    all_to_all x1, waiting for transfers between devices, body(): lax.all_to_all(joint, 'dec', split_axis=0, concat_axis=0, tiled=True)  27 us
    pallas_call x1, Pallas kernels, conv_call(): pl.pallas_call(conv_kernel, out_shape=(jax.ShapeDtypeStruct((streams, ste...  15.4 us
    all_to_all x1, starting transfers between devices, body(): lax.all_to_all(joint, 'dec', split_axis=0, concat_axis=0, tiled=True)  6.69 us
    unnamed x6, local copies, waits for them, and re-layouts  2.23 us
    pad x2, local copies, waits for them, and re-layouts, padded(): rows = jnp.pad(rows, ((0, extra), (0, 0)))  2.13 us
  transfers between devices with their start and end apart: 1, of which 1 were waited for; matrix products, arithmetic and copies ran while one was open for 1% of the time, Pallas kernels for 0%

profile of v5, /device:TPU:13, one launch (start us, length us, event | category | flops | bytes accessed | tf_op | source)
XLA Modules:
  0.0 63.7 jit_solution(15812354171619500690)
XLA Ops:
  0.6 0.7 %and_select_fusion.3 = (s32[128]{0:T(128)S(1)}, f32[128]{0:T(128)S(1)}) fusion(s32[128]{0:T(128)} %param.10), kind=kLoop, calls=%fused_computation.32 | loop fusion | flops 2688 | bytes 1536 | tf_op jit(solution)/shard_map/jit(floor_divide)/jit(_where)/select_n | solution.py:155
  1.3 1.1 %fusion.14 = (f32[1,128]{1,0:T(1,128)}, s32[128]{0:T(128)S(1)}, s32[128]{0:T(128)S(1)}) fusion(s32[]{:T(128)S(6)} %axis_index.12, s32[128]{0:T(128)} %param.11), kind=kLoop, calls=%fused_computation.43 | loop fusion | flops 2816 | bytes 2052 | tf_op jit(solution)/shard_map/reshape | solution.py:161
  2.5 0.1 fusion.1
  2.5 0.2 reduce_window_sum.18
  2.7 0.2 select_reduce_fusion
  2.9 0.1 multiply_reduce_fusion.1
  3.0 0.1 sub.35
  3.1 0.1 fusion.3
  3.2 0.2 reduce_window_sum.17
  3.4 0.2 select_reduce_fusion.1
  3.6 0.1 multiply_reduce_fusion
  3.7 0.1 sub.33
  3.8 0.1 fusion.10
  3.9 1.1 %copy.26 = bf16[16,8,4,512]{3,1,2,0:T(8,128)(2,1)S(1)} copy(bf16[16,8,4,512]{3,2,1,0:T(4,128)(2,1)} %bitcast.20) | data formatting | bytes 1048576
  5.1 0.0 copy-start
  5.1 0.4 convolution_convert_fusion.1
  5.5 0.3 reshape_reshape.6
  5.8 0.5 copy-done
  6.3 0.6 copy.24
  6.9 0.5 convolution_convert_fusion
  7.4 0.7 %reshape_reshape.7 = bf16[16,140,128]{2,1,0:T(8,128)(2,1)S(1)} reshape(bf16[80,3584]{1,0:T(8,128)(2,1)S(1)} %convolution_convert_fusion) | data formatting | bytes 1146880 | tf_op jit(solution)/shard_map/reshape;reshape | solution.py:177
  8.2 1.1 %pad_maximum_fusion = bf16[16,288,128]{2,1,0:T(8,128)(2,1)} fusion(bf16[16,4,128]{2,1,0:T(4,128)(2,1)S(1)} %reshape.60, bf16[16,140,128]{2,1,0:T(8,128)(2,1)S(1)} %reshape_reshape.7, bf16[16,144,128]{2,1,0:T(8,128)(2,1)S(1)} %reshape_reshape.6), kind=kLoop, calls=%fused_computation.2 | loop fusion | flops 3538944 | bytes 2359296 | tf_op jit(solution)/shard_map/concatenate | solution.py:174
  9.3 0.0 copy-start.1
  9.3 6.7 %all-to-all-start = ((bf16[16,288,128]{2,1,0:T(8,128)(2,1)}), bf16[16,288,128]{2,1,0:T(8,128)(2,1)S(1)}, u32[]{:S(2)}, u32[]{:S(2)}) async-start(bf16[16,288,128]{2,1,0:T(8,128)(2,1)} %pad_maximum_fusion), calls=%async_computation | async-start | bytes 2359296 | tf_op jit(solution)/shard_map/all_to_all | solution.py:182
  15.9 0.0 copy-done.1
  16.0 0.7 %copy.25.lim_ref = s32[128,1]{1,0:T(8,128)} copy(s32[128,1]{0,1:T(1,128)S(1)} %multiply_bitcast_fusion) | data formatting | bytes 1024 | tf_op jit(solution)/shard_map/reshape | solution.py:192
  16.7 27.0 %all-to-all-done = bf16[16,288,128]{2,1,0:T(8,128)(2,1)S(1)} async-done(((bf16[16,288,128]{2,1,0:T(8,128)(2,1)}), bf16[16,288,128]{2,1,0:T(8,128)(2,1)S(1)}, u32[]{:S(2)}, u32[]{:S(2)}) %all-to-all-start) | async-done | bytes 1179680 | tf_op jit(solution)/shard_map/all_to_all | solution.py:182
  43.7 0.1 slice.23
  43.8 0.1 reshape.66
  43.9 0.1 reshape.64
  44.0 0.6 pad_bitcast_fusion.clab_ref
  44.6 0.6 %reshape.61 = bf16[80,3584]{1,0:T(8,128)(2,1)S(1)} reshape(bf16[16,140,128]{2,1,0:T(8,128)(2,1)S(1)} %slice.20) | data formatting | bytes 1146880 | tf_op jit(solution)/shard_map/reshape | solution.py:184
  45.3 0.3 reshape.62
  45.6 1.0 %pad.22.crecv_ref = bf16[128,3584]{1,0:T(8,128)(2,1)} pad(bf16[80,3584]{1,0:T(8,128)(2,1)S(1)} %reshape.61, bf16[]{:T(256)} %constant.73.clone.1), padding=0_48x0_0 | pad | bytes 1490946 | tf_op jit(solution)/shard_map/jit(_pad)/pad | solution.py:137
  46.6 1.1 %pad.23.precv_ref = bf16[256,2048]{1,0:T(8,128)(2,1)} pad(bf16[144,2048]{1,0:T(8,128)(2,1)S(1)} %reshape.62, bf16[]{:T(256)} %constant.73.clone.1), padding=0_112x0_0 | pad | bytes 1638402 | tf_op jit(solution)/shard_map/jit(_pad)/pad | solution.py:137
  47.7 0.6 pad.25
  48.3 15.4 %shard_map.95 = (bf16[128,8,1024]{2,1,0:T(8,128)(2,1)}, bf16[7,128,512]{2,1,0:T(8,128)(2,1)}) custom-call(bf16[7,128,512]{2,1,0:T(8,128)(2,1)} %bitcast.17, bf16[128,3584]{1,0:T(8,128)(2,1)} %pad.22.crecv_ref, bf16[256,2048]{1,0:T(8,128)(2,1)} %pad.23.precv_ref, f32[1,128]{1,0:T(1,128)} %get-tuple-element.6.klab_ref, f32[1,128]{1,0:T(1,128)} %pad_bitcast_fusion.clab_ref, ...), custom_call_target="tpu_custom_call" | custom-call | tf_op jit(solution)/shard_map/pallas_call | solution.py:113
  (10 shorter events, 0.1 us)
Async XLA Ops:
  5.1 1.2 %copy-start = (bf16[128,7,512]{2,0,1:T(8,128)(2,1)S(1)}, bf16[128,7,512]{2,0,1:T(8,128)(2,1)}, u32[]{:S(2)}) copy-start(bf16[128,7,512]{2,0,1:T(8,128)(2,1)} %param.9) | copy-start | bytes 2752516
  9.3 6.7 %copy-start.1 = (s32[128]{0:T(128)S(1)}, s32[128]{0:T(128)}, u32[]{:S(2)}) copy-start(s32[128]{0:T(128)} %param.12) | copy-start | bytes 1540
  9.3 34.4 %all-to-all-start = ((bf16[16,288,128]{2,1,0:T(8,128)(2,1)}), bf16[16,288,128]{2,1,0:T(8,128)(2,1)S(1)}, u32[]{:S(2)}, u32[]{:S(2)}) async-start(bf16[16,288,128]{2,1,0:T(8,128)(2,1)} %pad_maximum_fusion), calls=%async_computation | async-start | bytes 2359296 | tf_op jit(solution)/shard_map/all_to_all | solution.py:182

commit v6 on v5

--- a/solution.py
+++ b/solution.py
@@ -133,9 +133,6 @@
 
 
 def padded(rows, labels):
-    extra = -rows.shape[0] % 128
-    rows = jnp.pad(rows, ((0, extra), (0, 0)))
-    labels = jnp.pad(labels, (0, extra), constant_values=-1.0)
     return rows, labels.reshape(1, -1)
 
 

time: 64 us -> 63.2 us (0.988)
    pad x3 -> x0, local copies, waits for them, and re-layouts: 2.7 us -> none  [the longest x2 2.13 us: padded(): rows = jnp.pad(rows, ((0, extra), (0, 0)))]
    another operation x0 -> x2, local copies, waits for them, and re-layouts: none -> 1.34 us  [padded(): return (rows, labels.reshape(1, -1))]
    reshape x1, local copies, waits for them, and re-layouts: 0.64 us -> 1.45 us  [body(): joint_recv[:, panel_rows:panel_rows + cache_rows]]
    reshape x1, local copies, waits for them, and re-layouts: 0.25 us -> 1.06 us  [body(): joint_recv[:, :panel_rows].reshape(number * pair_cap, panel_width)]
    reshape x3 -> x0, local copies, waits for them, and re-layouts: 0.77 us -> none  [the longest x1 0.6 us: padded(): return (rows, labels.reshape(1, -1))]
where the time goes in v6:
time: 63.2 us; the launch traced here: 62.9 us
  waiting for transfers between devices  27 us (43%)
  Pallas kernels  15.1 us (24%)
  local copies, waits for them, and re-layouts  8.17 us (13%)
  starting transfers between devices  6.69 us (11%)
  other arithmetic  4.15 us (7%)
  matrix products  0.94 us (1%)
  between operations  0.78 us (1%)
    all_to_all x1, waiting for transfers between devices, body(): lax.all_to_all(joint, 'dec', split_axis=0, concat_axis=0, tiled=True)  27 us
    pallas_call x1, Pallas kernels, conv_call(): pl.pallas_call(conv_kernel, out_shape=(jax.ShapeDtypeStruct((streams, ste...  15.1 us
    all_to_all x1, starting transfers between devices, body(): lax.all_to_all(joint, 'dec', split_axis=0, concat_axis=0, tiled=True)  6.69 us
    unnamed x6, local copies, waits for them, and re-layouts  2.23 us
    reshape x1, local copies, waits for them, and re-layouts, body(): joint_recv[:, panel_rows:panel_rows + cache_rows]  1.45 us
    another operation x2, local copies, waits for them, and re-layouts, padded(): return (rows, labels.reshape(1, -1))  1.34 us
  transfers between devices with their start and end apart: 1, of which 1 were waited for; matrix products, arithmetic and copies ran while one was open for 1% of the time, Pallas kernels for 0%

profile of v6, /device:TPU:13, one launch (start us, length us, event | category | flops | bytes accessed | tf_op | source)
XLA Modules:
  0.0 62.9 jit_solution(8684986319826194451)
XLA Ops:
  0.6 0.7 %and_select_fusion.3 = (s32[128]{0:T(128)S(1)}, f32[128]{0:T(128)S(1)}) fusion(s32[128]{0:T(128)} %param.10), kind=kLoop, calls=%fused_computation.32 | loop fusion | flops 2688 | bytes 1536 | tf_op jit(solution)/shard_map/jit(floor_divide)/jit(_where)/select_n | solution.py:152
  1.3 1.2 %fusion.14 = (f32[1,128]{1,0:T(1,128)}, s32[128]{0:T(128)S(1)}, s32[128]{0:T(128)S(1)}) fusion(s32[]{:T(128)S(6)} %axis_index.12, s32[128]{0:T(128)} %param.11), kind=kLoop, calls=%fused_computation.43 | loop fusion | flops 2816 | bytes 2052 | tf_op jit(solution)/shard_map/reshape | solution.py:158
  2.5 0.1 fusion.1
  2.6 0.2 reduce_window_sum.18
  2.7 0.2 select_reduce_fusion
  2.9 0.1 multiply_reduce_fusion.1
  3.1 0.1 sub.35
  3.1 0.1 fusion.3
  3.2 0.2 reduce_window_sum.17
  3.4 0.2 select_reduce_fusion.1
  3.6 0.1 multiply_reduce_fusion
  3.7 0.1 sub.33
  3.8 0.1 fusion.10
  3.9 1.1 %copy.26 = bf16[16,8,4,512]{3,1,2,0:T(8,128)(2,1)S(1)} copy(bf16[16,8,4,512]{3,2,1,0:T(4,128)(2,1)} %bitcast.17) | data formatting | bytes 1048576
  5.1 0.0 copy-start
  5.1 0.4 convolution_convert_fusion.1
  5.5 0.3 reshape_reshape.12
  5.8 0.5 copy-done
  6.3 0.6 copy.24
  6.9 0.5 convolution_convert_fusion
  7.4 0.7 %reshape_reshape.13 = bf16[16,140,128]{2,1,0:T(8,128)(2,1)S(1)} reshape(bf16[80,3584]{1,0:T(8,128)(2,1)S(1)} %convolution_convert_fusion) | data formatting | bytes 1146880 | tf_op jit(solution)/shard_map/reshape;reshape | solution.py:174
  8.2 1.1 %pad_maximum_fusion = bf16[16,288,128]{2,1,0:T(8,128)(2,1)} fusion(bf16[16,4,128]{2,1,0:T(4,128)(2,1)S(1)} %reshape.48, bf16[16,140,128]{2,1,0:T(8,128)(2,1)S(1)} %reshape_reshape.13, bf16[16,144,128]{2,1,0:T(8,128)(2,1)S(1)} %reshape_reshape.12), kind=kLoop, calls=%fused_computation.2 | loop fusion | flops 3538944 | bytes 2359296 | tf_op jit(solution)/shard_map/concatenate | solution.py:171
  9.3 0.0 copy-start.1
  9.3 6.7 %all-to-all-start = ((bf16[16,288,128]{2,1,0:T(8,128)(2,1)}), bf16[16,288,128]{2,1,0:T(8,128)(2,1)S(1)}, u32[]{:S(2)}, u32[]{:S(2)}) async-start(bf16[16,288,128]{2,1,0:T(8,128)(2,1)} %pad_maximum_fusion), calls=%async_computation | async-start | bytes 2359296 | tf_op jit(solution)/shard_map/all_to_all | solution.py:179
  16.0 0.0 copy-done.1
  16.0 0.7 %copy.25.lim_ref = s32[128,1]{1,0:T(8,128)} copy(s32[128,1]{0,1:T(1,128)S(1)} %multiply_bitcast_fusion) | data formatting | bytes 1024 | tf_op jit(solution)/shard_map/reshape | solution.py:189
  16.7 27.0 %all-to-all-done = bf16[16,288,128]{2,1,0:T(8,128)(2,1)S(1)} async-done(((bf16[16,288,128]{2,1,0:T(8,128)(2,1)}), bf16[16,288,128]{2,1,0:T(8,128)(2,1)S(1)}, u32[]{:S(2)}, u32[]{:S(2)}) %all-to-all-start) | async-done | bytes 1179680 | tf_op jit(solution)/shard_map/all_to_all | solution.py:179
  43.7 0.1 slice.23
  43.8 0.7 %reshape_reshape.15.plab_ref = f32[1,144]{1,0:T(1,128)} reshape(f32[16,9]{1,0:T(8,128)S(1)} %bitcast.19) | data formatting | bytes 1152 | tf_op jit(solution)/shard_map/reshape;reshape | solution.py:136
  44.5 0.7 %reshape_reshape.14.clab_ref = f32[1,80]{1,0:T(1,128)} reshape(f32[16,5]{1,0:T(8,128)S(1)} %slice.23) | data formatting | bytes 640 | tf_op jit(solution)/shard_map/reshape;reshape | solution.py:136
  45.2 1.5 %reshape.49.crecv_ref = bf16[80,3584]{1,0:T(8,128)(2,1)} reshape(bf16[16,140,128]{2,1,0:T(8,128)(2,1)S(1)} %slice.20) | data formatting | bytes 1146880 | tf_op jit(solution)/shard_map/reshape | solution.py:181
  46.7 1.1 %reshape.50.precv_ref = bf16[144,2048]{1,0:T(8,128)(2,1)} reshape(bf16[16,144,128]{2,1,0:T(8,128)(2,1)S(1)} %slice.21) | data formatting | bytes 1179648 | tf_op jit(solution)/shard_map/reshape | solution.py:180
  47.7 15.1 %shard_map.95 = (bf16[128,8,1024]{2,1,0:T(8,128)(2,1)}, bf16[7,128,512]{2,1,0:T(8,128)(2,1)}) custom-call(bf16[7,128,512]{2,1,0:T(8,128)(2,1)} %bitcast.15, bf16[80,3584]{1,0:T(8,128)(2,1)} %reshape.49.crecv_ref, bf16[144,2048]{1,0:T(8,128)(2,1)} %reshape.50.precv_ref, f32[1,128]{1,0:T(1,128)} %get-tuple-element.6.klab_ref, ...), custom_call_target="tpu_custom_call" | custom-call | tf_op jit(solution)/shard_map/pallas_call | solution.py:113
  (10 shorter events, 0.1 us)
Async XLA Ops:
  5.1 1.2 %copy-start = (bf16[128,7,512]{2,0,1:T(8,128)(2,1)S(1)}, bf16[128,7,512]{2,0,1:T(8,128)(2,1)}, u32[]{:S(2)}) copy-start(bf16[128,7,512]{2,0,1:T(8,128)(2,1)} %param.9) | copy-start | bytes 2752516
  9.3 6.7 %copy-start.1 = (s32[128]{0:T(128)S(1)}, s32[128]{0:T(128)}, u32[]{:S(2)}) copy-start(s32[128]{0:T(128)} %param.12) | copy-start | bytes 1540
  9.3 34.4 %all-to-all-start = ((bf16[16,288,128]{2,1,0:T(8,128)(2,1)}), bf16[16,288,128]{2,1,0:T(8,128)(2,1)S(1)}, u32[]{:S(2)}, u32[]{:S(2)}) async-start(bf16[16,288,128]{2,1,0:T(8,128)(2,1)} %pad_maximum_fusion), calls=%async_computation | async-start | bytes 2359296 | tf_op jit(solution)/shard_map/all_to_all | solution.py:179

commit v7 on v4

--- a/solution.py
+++ b/solution.py
@@ -10,8 +10,10 @@
 
 
 def buckets(rows, target, local, capacity, number):
-    hits = (target[:, None] == jnp.arange(number, dtype=jnp.int32)[None, :]).astype(jnp.int32)
-    rank = jnp.sum(hits * (jnp.cumsum(hits, axis=0) - 1), axis=1)
+    count = target.shape[0]
+    line = lax.broadcasted_iota(jnp.int32, (count, count), 0)
+    column = lax.broadcasted_iota(jnp.int32, (count, count), 1)
+    rank = jnp.sum(((target[None, :] == target[:, None]) & (column < line)).astype(jnp.int32), axis=1)
     place = jnp.where(target >= 0, target * capacity + rank, -1)
     picker = (place[:, None] == jnp.arange(number * capacity, dtype=jnp.int32)[None, :]).astype(
         jnp.bfloat16
@@ -125,10 +127,10 @@
     cache_width = rows_kept * channels
     flat_latents = latents.reshape(streams, panel_width)
     flat_cache = cache.reshape(streams, cache_width)
-    panel_owner = panel_slot // streams
-    panel_local = panel_slot % streams
-    cache_owner = cache_slot // streams
-    cache_local = cache_slot % streams
+    panel_owner = lax.div(panel_slot, streams)
+    panel_local = lax.rem(panel_slot, streams)
+    cache_owner = lax.div(cache_slot, streams)
+    cache_local = lax.rem(cache_slot, streams)
     moving = cache_owner != myself
     staying = jnp.logical_not(moving)
     stay_pick = (

time: 62.4 us -> 61.3 us (0.982)
  other arithmetic: 4.3 us -> 3.22 us
    select_n x2 -> x0, other arithmetic: 0.67 us -> none  [the longest x1 0.67 us: body(): panel_owner = panel_slot // streams]
    div x0 -> x1, other arithmetic: none -> 0.67 us  [body(): panel_owner = lax.div(panel_slot, streams)]
    not x1, other arithmetic: 0.67 us -> 0.01 us  [body(): staying = jnp.logical_not(moving)]
    unnamed x6 -> x8, local copies, waits for them, and re-layouts: 1.78 us -> 1.78 us
where the time goes in v7:
time: 61.3 us; the launch traced here: 61.1 us
  waiting for transfers between devices  27 us (44%)
  Pallas kernels  14.4 us (23%)
  starting transfers between devices  6.56 us (11%)
  local copies, waits for them, and re-layouts  4.94 us (8%)
  matrix products  4.11 us (7%)
  other arithmetic  3.22 us (5%)
  between operations  0.83 us (1%)
    all_to_all x1, waiting for transfers between devices, body(): lax.all_to_all(joint, 'dec', split_axis=0, concat_axis=0, tiled=True)  27 us
    pallas_call x1, Pallas kernels, conv_call(): pl.pallas_call(conv_kernel, out_shape=(jax.ShapeDtypeStruct((streams, ste...  14.4 us
    all_to_all x1, starting transfers between devices, body(): lax.all_to_all(joint, 'dec', split_axis=0, concat_axis=0, tiled=True)  6.56 us
    unnamed x8, local copies, waits for them, and re-layouts  1.78 us
    dot_general x2, matrix products, settle(): return jnp.dot(picker.T, received, preferred_element_type=jnp.float32)  1.72 us
    dot_general x1, matrix products, body(): kept = jnp.dot(stay_pick.T, flat_cache, preferred_element_type=jnp.float32)  1.45 us
  transfers between devices with their start and end apart: 1, of which 1 were waited for; matrix products, arithmetic and copies ran while one was open for 1% of the time, Pallas kernels for 0%

profile of v7, /device:TPU:13, one launch (start us, length us, event | category | flops | bytes accessed | tf_op | source)
XLA Modules:
  0.0 61.1 jit_solution(16991379086351023069)
XLA Ops:
  0.6 0.0 copy-start
  0.6 0.7 %add_convert_fusion.2 = (f32[128]{0:T(128)S(1)}, s32[128]{0:T(128)S(1)}, s32[128]{0:T(128)S(1)}) fusion(s32[128]{0:T(128)} %param.11, s32[]{:T(128)S(6)} %axis_index.12), kind=kLoop, calls=%fused_computation.50 | loop fusion | flops 1664 | bytes 2052 | tf_op jit(solution)/shard_map/convert_element_type | solution.py:23
  1.4 0.2 convert_reduce_fusion
  1.6 0.1 multiply_reduce_fusion.1
  1.7 0.7 %compare_select_fusion.4 = (s32[128]{0:T(128)S(1)}, f32[128]{0:T(128)S(1)}) fusion(s32[128]{0:T(128)} %param.10), kind=kLoop, calls=%fused_computation.42 | loop fusion | flops 1408 | bytes 1536 | tf_op jit(solution)/shard_map/div | solution.py:130
  2.4 0.2 convert_reduce_fusion.1
  2.6 0.1 multiply_reduce_fusion
  2.7 0.1 sub.13
  2.8 0.1 sub.15
  2.9 0.1 fusion.19
  3.0 1.1 %copy.17 = bf16[16,8,4,512]{3,1,2,0:T(8,128)(2,1)S(1)} copy(bf16[16,8,4,512]{3,2,1,0:T(4,128)(2,1)} %bitcast.17) | data formatting | bytes 1048576
  4.1 0.4 convolution_convert_fusion.1
  4.6 0.3 reshape_reshape.6
  4.8 0.0 copy-done
  4.9 0.6 %copy.15 = bf16[128,7,512]{0,2,1:T(8,128)(2,1)S(1)} copy(bf16[128,7,512]{2,0,1:T(8,128)(2,1)S(1)} %copy-done) | data formatting | bytes 1835008 | tf_op args[1]
  5.5 0.5 convolution_convert_fusion
  6.0 0.7 %reshape_reshape.7 = bf16[16,140,128]{2,1,0:T(8,128)(2,1)S(1)} reshape(bf16[80,3584]{1,0:T(8,128)(2,1)S(1)} %convolution_convert_fusion) | data formatting | bytes 1146880 | tf_op jit(solution)/shard_map/reshape;reshape | solution.py:155
  6.8 0.0 copy-start.2
  6.8 0.0 copy-start.1
  6.8 1.1 %pad_maximum_fusion = bf16[16,288,128]{2,1,0:T(8,128)(2,1)} fusion(bf16[16,4,128]{2,1,0:T(4,128)(2,1)S(1)} %reshape.51, bf16[16,140,128]{2,1,0:T(8,128)(2,1)S(1)} %reshape_reshape.7, bf16[16,144,128]{2,1,0:T(8,128)(2,1)S(1)} %reshape_reshape.6), kind=kLoop, calls=%fused_computation.5 | loop fusion | flops 3538944 | bytes 2359296 | tf_op jit(solution)/shard_map/concatenate | solution.py:152
  7.9 6.6 %all-to-all-start = ((bf16[16,288,128]{2,1,0:T(8,128)(2,1)}), bf16[16,288,128]{2,1,0:T(8,128)(2,1)S(1)}, u32[]{:S(2)}, u32[]{:S(2)}) async-start(bf16[16,288,128]{2,1,0:T(8,128)(2,1)} %pad_maximum_fusion), calls=%async_computation | async-start | bytes 2359296 | tf_op jit(solution)/shard_map/all_to_all | solution.py:160
  14.5 0.0 copy-done.2
  14.5 0.7 %copy.16.lim_ref = s32[128,1]{1,0:T(8,128)} copy(s32[128,1]{0,1:T(1,128)S(1)} %multiply_bitcast_fusion) | data formatting | bytes 1024 | tf_op jit(solution)/shard_map/reshape | solution.py:171
  15.2 0.0 copy-done.1
  15.2 27.0 %all-to-all-done = bf16[16,288,128]{2,1,0:T(8,128)(2,1)S(1)} async-done(((bf16[16,288,128]{2,1,0:T(8,128)(2,1)}), bf16[16,288,128]{2,1,0:T(8,128)(2,1)S(1)}, u32[]{:S(2)}, u32[]{:S(2)}) %all-to-all-start) | async-done | bytes 1179680 | tf_op jit(solution)/shard_map/all_to_all | solution.py:160
  42.2 0.1 slice.21
  42.3 0.1 eq.134
  42.4 0.1 eq.130
  42.5 0.6 %reshape.52 = bf16[80,3584]{1,0:T(8,128)(2,1)S(1)} reshape(bf16[16,140,128]{2,1,0:T(8,128)(2,1)S(1)} %slice.22) | data formatting | bytes 1146880 | tf_op jit(solution)/shard_map/reshape | solution.py:162
  43.2 0.3 reshape.53
  43.5 1.2 %convolution_convert_fusion.2.pan_ref = bf16[128,2048]{1,0:T(8,128)(2,1)} fusion(bf16[144,2048]{1,0:T(8,128)(2,1)S(1)} %reshape.53, f32[144]{0:T(256)S(1)} %eq.134), kind=kOutput, calls=%fused_computation.4 | convolution fusion | flops 75778048 | bytes 1114688 | tf_op jit(solution)/shard_map/dot_general | solution.py:37
  44.7 0.5 fusion.9
  45.2 1.5 %fusion.own_ref = bf16[128,3584]{1,0:T(8,128)(2,1)} fusion(f32[128,3584]{1,0:T(8,128)S(1)} %fusion.9, bf16[128,3584]{0,1:T(8,128)(2,1)S(1)} %bitcast.15, s32[128]{0:T(128)S(1)} %get-tuple-element.7, pred[128]{0:T(512)(128)(4,1)S(1)} %compare_not_fusion), kind=kOutput, calls=%fused_computation.1 | convolution fusion | flops 118407168 | bytes 3670656 | tf_op jit(solution)/shard_map/dot_general | solution.py:139
  46.7 14.4 %shard_map.119 = (bf16[128,8,1024]{2,1,0:T(8,128)(2,1)}, bf16[7,128,512]{2,1,0:T(8,128)(2,1)}) custom-call(bf16[128,3584]{1,0:T(8,128)(2,1)} %fusion.own_ref, bf16[128,2048]{1,0:T(8,128)(2,1)} %convolution_convert_fusion.2.pan_ref, f32[4,512]{1,0:T(4,128)} %uw_ref.1, bf16[7,512,1024]{2,1,0:T(8,128)(2,1)} %w_ref.1, f32[1,1024]{1,0:T(1,128)} %bitcast.20, ...), custom_call_target="tpu_custom_call" | custom-call | tf_op jit(solution)/shard_map/pallas_call | solution.py:93
  (10 shorter events, 0.1 us)
Async XLA Ops:
  0.6 4.2 %copy-start = (bf16[128,7,512]{2,0,1:T(8,128)(2,1)S(1)}, bf16[128,7,512]{2,0,1:T(8,128)(2,1)}, u32[]{:S(2)}) copy-start(bf16[128,7,512]{2,0,1:T(8,128)(2,1)} %param.9) | copy-start | bytes 2752516
  6.8 7.7 %copy-start.2 = (s32[128]{0:T(128)S(1)}, s32[128]{0:T(128)}, u32[]{:S(2)}) copy-start(s32[128]{0:T(128)} %param.12) | copy-start | bytes 1540
  6.8 8.4 %copy-start.1 = (s32[128]{0:T(128)S(1)}, s32[128]{0:T(128)}, u32[]{:S(2)}) copy-start(s32[128]{0:T(128)} %param.11) | copy-start | bytes 1540
  7.9 34.3 %all-to-all-start = ((bf16[16,288,128]{2,1,0:T(8,128)(2,1)}), bf16[16,288,128]{2,1,0:T(8,128)(2,1)S(1)}, u32[]{:S(2)}, u32[]{:S(2)}) async-start(bf16[16,288,128]{2,1,0:T(8,128)(2,1)} %pad_maximum_fusion), calls=%async_computation | async-start | bytes 2359296 | tf_op jit(solution)/shard_map/all_to_all | solution.py:160

commit v8 on v7

--- a/solution.py
+++ b/solution.py
@@ -77,7 +77,7 @@
         part = jnp.dot(window, w_ref[tap], preferred_element_type=jnp.float32)
         acc = part if acc is None else acc + part
     acc = acc + b_ref[...]
-    act = jnp.where(acc > 0, acc, jnp.exp(jnp.minimum(acc, 0.0)) - 1.0)
+    act = jnp.where(acc > 0, acc, jnp.exp(acc) - 1.0)
     act = act.reshape(steps, streams, block)
     for step in range(steps):
         o_ref[:, step, :] = jnp.where(step < lim, act[step], 0.0).astype(o_ref.dtype)
@@ -136,7 +136,9 @@
     stay_pick = (
         staying[:, None] & (cache_local[:, None] == jnp.arange(streams, dtype=jnp.int32)[None, :])
     ).astype(jnp.bfloat16)
-    kept = jnp.dot(stay_pick.T, flat_cache, preferred_element_type=jnp.float32)
+    kept = lax.optimization_barrier(
+        jnp.dot(stay_pick.T, flat_cache, preferred_element_type=jnp.float32).astype(jnp.bfloat16)
+    )
     cache_send, cache_labels = buckets(
         flat_cache, jnp.where(moving, cache_owner, -1), cache_local, mig_cap, number
     )
@@ -167,7 +169,7 @@
     cache_rl = recv_labels[:, pair_cap : pair_cap + mig_cap].reshape(-1)
     panels = settle(panel_recv, panel_rl, streams).astype(jnp.bfloat16)
     arrived = settle(cache_recv, cache_rl, streams)
-    owned = (kept + arrived).astype(jnp.bfloat16)
+    owned = (kept.astype(jnp.float32) + arrived).astype(jnp.bfloat16)
     limit = (2 * frames_valid).reshape(streams, 1)
     decoded, new_cache = conv_call(
         owned, panels, up_weight, conv_weight, conv_bias, limit, 2 * frames

time: 61.3 us -> 60.7 us (level)
    dot_general x2, matrix products: 1.72 us -> 2.65 us  [settle(): return jnp.dot(picker.T, received, preferred_element_type=jnp.float32)]
    dot_general x1, matrix products: 1.45 us -> 0.52 us  [body(): jnp.dot(stay_pick.T, flat_cache, preferred_element_type=jnp.float32)]
  transfers between devices with their start and end apart: 1 -> 1, of which waited for: 1 -> 1; matrix products, arithmetic and copies ran while one was open for 1% -> 2% of each run, Pallas kernels for 0% -> 0%
where the time goes in v8:
time: 60.7 us; the launch traced here: 60.4 us
  waiting for transfers between devices  26.5 us (44%)
  Pallas kernels  14.3 us (24%)
  starting transfers between devices  6.56 us (11%)
  local copies, waits for them, and re-layouts  4.94 us (8%)
  matrix products  4.12 us (7%)
  other arithmetic  3.22 us (5%)
  between operations  0.83 us (1%)
    all_to_all x1, waiting for transfers between devices, body(): lax.all_to_all(joint, 'dec', split_axis=0, concat_axis=0, tiled=True)  26.5 us
    pallas_call x1, Pallas kernels, conv_call(): pl.pallas_call(conv_kernel, out_shape=(jax.ShapeDtypeStruct((streams, ste...  14.3 us
    all_to_all x1, starting transfers between devices, body(): lax.all_to_all(joint, 'dec', split_axis=0, concat_axis=0, tiled=True)  6.56 us
    dot_general x2, matrix products, settle(): return jnp.dot(picker.T, received, preferred_element_type=jnp.float32)  2.65 us
    unnamed x8, local copies, waits for them, and re-layouts  1.78 us
  transfers between devices with their start and end apart: 1, of which 1 were waited for; matrix products, arithmetic and copies ran while one was open for 2% of the time, Pallas kernels for 0%

profile of v8, /device:TPU:13, one launch (start us, length us, event | category | flops | bytes accessed | tf_op | source)
XLA Modules:
  0.0 60.4 jit_solution(7889554734055151212)
XLA Ops:
  0.6 0.0 copy-start
  0.6 0.7 %add_convert_fusion.2 = (f32[128]{0:T(128)S(1)}, s32[128]{0:T(128)S(1)}, s32[128]{0:T(128)S(1)}) fusion(s32[128]{0:T(128)} %param.11, s32[]{:T(128)S(6)} %axis_index.12), kind=kLoop, calls=%fused_computation.50 | loop fusion | flops 1664 | bytes 2052 | tf_op jit(solution)/shard_map/convert_element_type | solution.py:23
  1.4 0.2 convert_reduce_fusion
  1.6 0.1 multiply_reduce_fusion.1
  1.7 0.7 %compare_select_fusion.4 = (s32[128]{0:T(128)S(1)}, f32[128]{0:T(128)S(1)}) fusion(s32[128]{0:T(128)} %param.10), kind=kLoop, calls=%fused_computation.42 | loop fusion | flops 1408 | bytes 1536 | tf_op jit(solution)/shard_map/div | solution.py:130
  2.4 0.2 convert_reduce_fusion.1
  2.6 0.1 multiply_reduce_fusion
  2.7 0.1 sub.13
  2.8 0.1 sub.15
  2.9 0.1 fusion.18
  3.0 1.1 %copy.17 = bf16[16,8,4,512]{3,1,2,0:T(8,128)(2,1)S(1)} copy(bf16[16,8,4,512]{3,2,1,0:T(4,128)(2,1)} %bitcast.17) | data formatting | bytes 1048576
  4.1 0.4 convolution_convert_fusion.2
  4.6 0.3 reshape_reshape.6
  4.8 0.0 copy-done
  4.9 0.6 %copy.15 = bf16[128,7,512]{0,2,1:T(8,128)(2,1)S(1)} copy(bf16[128,7,512]{2,0,1:T(8,128)(2,1)S(1)} %copy-done) | data formatting | bytes 1835008 | tf_op args[1]
  5.5 0.5 convolution_convert_fusion.1
  6.0 0.7 %reshape_reshape.7 = bf16[16,140,128]{2,1,0:T(8,128)(2,1)S(1)} reshape(bf16[80,3584]{1,0:T(8,128)(2,1)S(1)} %convolution_convert_fusion.1) | data formatting | bytes 1146880 | tf_op jit(solution)/shard_map/reshape;reshape | solution.py:157
  6.8 0.0 copy-start.2
  6.8 0.0 copy-start.1
  6.8 1.1 %pad_maximum_fusion = bf16[16,288,128]{2,1,0:T(8,128)(2,1)} fusion(bf16[16,4,128]{2,1,0:T(4,128)(2,1)S(1)} %reshape.51, bf16[16,140,128]{2,1,0:T(8,128)(2,1)S(1)} %reshape_reshape.7, bf16[16,144,128]{2,1,0:T(8,128)(2,1)S(1)} %reshape_reshape.6), kind=kLoop, calls=%fused_computation.6 | loop fusion | flops 3538944 | bytes 2359296 | tf_op jit(solution)/shard_map/concatenate | solution.py:154
  7.9 6.6 %all-to-all-start = ((bf16[16,288,128]{2,1,0:T(8,128)(2,1)}), bf16[16,288,128]{2,1,0:T(8,128)(2,1)S(1)}, u32[]{:S(2)}, u32[]{:S(2)}) async-start(bf16[16,288,128]{2,1,0:T(8,128)(2,1)} %pad_maximum_fusion), calls=%async_computation | async-start | bytes 2359296 | tf_op jit(solution)/shard_map/all_to_all | solution.py:162
  14.5 0.0 copy-done.2
  14.5 0.7 %copy.16.lim_ref = s32[128,1]{1,0:T(8,128)} copy(s32[128,1]{0,1:T(1,128)S(1)} %multiply_bitcast_fusion) | data formatting | bytes 1024 | tf_op jit(solution)/shard_map/reshape | solution.py:173
  15.2 0.0 copy-done.1
  15.2 0.5 convolution_convert_fusion
  15.7 26.5 %all-to-all-done = bf16[16,288,128]{2,1,0:T(8,128)(2,1)S(1)} async-done(((bf16[16,288,128]{2,1,0:T(8,128)(2,1)}), bf16[16,288,128]{2,1,0:T(8,128)(2,1)S(1)}, u32[]{:S(2)}, u32[]{:S(2)}) %all-to-all-start) | async-done | bytes 1179680 | tf_op jit(solution)/shard_map/all_to_all | solution.py:162
  42.2 0.1 slice.21
  42.3 0.1 eq.134
  42.4 0.1 eq.130
  42.5 0.6 %reshape.52 = bf16[80,3584]{1,0:T(8,128)(2,1)S(1)} reshape(bf16[16,140,128]{2,1,0:T(8,128)(2,1)S(1)} %slice.22) | data formatting | bytes 1146880 | tf_op jit(solution)/shard_map/reshape | solution.py:164
  43.2 0.3 reshape.53
  43.5 1.2 %convolution_convert_fusion.3.pan_ref = bf16[128,2048]{1,0:T(8,128)(2,1)} fusion(bf16[144,2048]{1,0:T(8,128)(2,1)S(1)} %reshape.53, f32[144]{0:T(256)S(1)} %eq.134), kind=kOutput, calls=%fused_computation.5 | convolution fusion | flops 75778048 | bytes 1114688 | tf_op jit(solution)/shard_map/dot_general | solution.py:37
  44.7 1.4 %fusion.own_ref = bf16[128,3584]{1,0:T(8,128)(2,1)} fusion(bf16[80,3584]{1,0:T(8,128)(2,1)S(1)} %reshape.52, bf16[128,3584]{1,0:T(8,128)(2,1)S(1)} %convolution_convert_fusion, f32[80]{0:T(128)S(1)} %eq.130), kind=kOutput, calls=%fused_computation.1 | convolution fusion | flops 74786816 | bytes 2408768 | tf_op jit(solution)/shard_map/dot_general | solution.py:37
  46.1 14.3 %shard_map.119 = (bf16[128,8,1024]{2,1,0:T(8,128)(2,1)}, bf16[7,128,512]{2,1,0:T(8,128)(2,1)}) custom-call(bf16[128,3584]{1,0:T(8,128)(2,1)} %fusion.own_ref, bf16[128,2048]{1,0:T(8,128)(2,1)} %convolution_convert_fusion.3.pan_ref, f32[4,512]{1,0:T(4,128)} %uw_ref.1, bf16[7,512,1024]{2,1,0:T(8,128)(2,1)} %w_ref.1, f32[1,1024]{1,0:T(1,128)} %bitcast.20, ...), custom_call_target="tpu_custom_call" | custom-call | tf_op jit(solution)/shard_map/pallas_call | solution.py:93
  (10 shorter events, 0.1 us)
Async XLA Ops:
  0.6 4.2 %copy-start = (bf16[128,7,512]{2,0,1:T(8,128)(2,1)S(1)}, bf16[128,7,512]{2,0,1:T(8,128)(2,1)}, u32[]{:S(2)}) copy-start(bf16[128,7,512]{2,0,1:T(8,128)(2,1)} %param.9) | copy-start | bytes 2752516
  6.8 7.7 %copy-start.2 = (s32[128]{0:T(128)S(1)}, s32[128]{0:T(128)}, u32[]{:S(2)}) copy-start(s32[128]{0:T(128)} %param.12) | copy-start | bytes 1540
  6.8 8.4 %copy-start.1 = (s32[128]{0:T(128)S(1)}, s32[128]{0:T(128)}, u32[]{:S(2)}) copy-start(s32[128]{0:T(128)} %param.11) | copy-start | bytes 1540
  7.9 34.3 %all-to-all-start = ((bf16[16,288,128]{2,1,0:T(8,128)(2,1)}), bf16[16,288,128]{2,1,0:T(8,128)(2,1)S(1)}, u32[]{:S(2)}, u32[]{:S(2)}) async-start(bf16[16,288,128]{2,1,0:T(8,128)(2,1)} %pad_maximum_fusion), calls=%async_computation | async-start | bytes 2359296 | tf_op jit(solution)/shard_map/all_to_all | solution.py:162

commit v9 on v8

--- a/solution.py
+++ b/solution.py
@@ -127,10 +127,12 @@
     cache_width = rows_kept * channels
     flat_latents = latents.reshape(streams, panel_width)
     flat_cache = cache.reshape(streams, cache_width)
-    panel_owner = lax.div(panel_slot, streams)
-    panel_local = lax.rem(panel_slot, streams)
-    cache_owner = lax.div(cache_slot, streams)
-    cache_local = lax.rem(cache_slot, streams)
+    slots = jnp.stack([panel_slot, cache_slot, frames_valid])
+    owners = lax.div(slots, streams)
+    locals_ = lax.rem(slots, streams)
+    panel_owner, cache_owner = owners[0], owners[1]
+    panel_local, cache_local = locals_[0], locals_[1]
+    frames_valid = slots[2]
     moving = cache_owner != myself
     staying = jnp.logical_not(moving)
     stay_pick = (

time: 60.7 us -> 60 us (0.988)
  other arithmetic: 3.22 us -> 2.6 us
    convert_element_type x1 -> x0, other arithmetic: 0.74 us -> none  [buckets(): (local + 1).astype(jnp.float32)[None, :]]
    unnamed x8 -> x6, local copies, waits for them, and re-layouts: 1.78 us -> 1.77 us
where the time goes in v9:
time: 60 us; the launch traced here: 59.8 us
  waiting for transfers between devices  26.5 us (44%)
  Pallas kernels  14.3 us (24%)
  starting transfers between devices  6.56 us (11%)
  local copies, waits for them, and re-layouts  4.93 us (8%)
  matrix products  4.12 us (7%)
  other arithmetic  2.6 us (4%)
  between operations  0.83 us (1%)
    all_to_all x1, waiting for transfers between devices, body(): lax.all_to_all(joint, 'dec', split_axis=0, concat_axis=0, tiled=True)  26.5 us
    pallas_call x1, Pallas kernels, conv_call(): pl.pallas_call(conv_kernel, out_shape=(jax.ShapeDtypeStruct((streams, ste...  14.3 us
    all_to_all x1, starting transfers between devices, body(): lax.all_to_all(joint, 'dec', split_axis=0, concat_axis=0, tiled=True)  6.56 us
    dot_general x2, matrix products, settle(): return jnp.dot(picker.T, received, preferred_element_type=jnp.float32)  2.65 us
    unnamed x6, local copies, waits for them, and re-layouts  1.77 us
  transfers between devices with their start and end apart: 1, of which 1 were waited for; matrix products, arithmetic and copies ran while one was open for 2% of the time, Pallas kernels for 0%

profile of v9, /device:TPU:13, one launch (start us, length us, event | category | flops | bytes accessed | tf_op | source)
XLA Modules:
  0.0 59.8 jit_solution(5365910256869231072)
XLA Ops:
  0.6 0.0 copy-start
  0.6 0.8 %negate_select_fusion.1 = (s32[3,128]{1,0:T(4,128)S(1)}, s32[3,128]{1,0:T(4,128)S(1)}) fusion(s32[1,128]{1,0:T(1,128)} %bitcast.41, s32[1,128]{1,0:T(1,128)} %bitcast.39, s32[1,128]{1,0:T(1,128)} %bitcast.40), kind=kLoop, calls=%fused_computation.38 | loop fusion | flops 4224 | bytes 4608 | tf_op jit(solution)/shard_map/div | solution.py:131
  1.4 0.2 convert_reduce_fusion.1
  1.6 0.2 convert_reduce_fusion
  1.8 0.1 multiply_reduce_fusion.1
  1.9 0.1 multiply_reduce_fusion
  2.1 0.1 sub.13
  2.2 0.1 sub.15
  2.3 0.1 fusion.18
  2.4 1.1 %copy.17 = bf16[16,8,4,512]{3,1,2,0:T(8,128)(2,1)S(1)} copy(bf16[16,8,4,512]{3,2,1,0:T(4,128)(2,1)} %bitcast.35) | data formatting | bytes 1048576
  3.5 0.4 convolution_convert_fusion.2
  4.0 0.3 reshape_reshape.6
  4.2 0.0 copy-done
  4.2 0.6 %copy.15 = bf16[128,7,512]{0,2,1:T(8,128)(2,1)S(1)} copy(bf16[128,7,512]{2,0,1:T(8,128)(2,1)S(1)} %copy-done) | data formatting | bytes 1835008 | tf_op args[1]
  4.9 0.5 convolution_convert_fusion.1
  5.4 0.7 %reshape_reshape.7 = bf16[16,140,128]{2,1,0:T(8,128)(2,1)S(1)} reshape(bf16[80,3584]{1,0:T(8,128)(2,1)S(1)} %convolution_convert_fusion.1) | data formatting | bytes 1146880 | tf_op jit(solution)/shard_map/reshape;reshape | solution.py:159
  6.2 0.0 copy-start.1
  6.2 1.1 %pad_maximum_fusion = bf16[16,288,128]{2,1,0:T(8,128)(2,1)} fusion(bf16[16,4,128]{2,1,0:T(4,128)(2,1)S(1)} %reshape.80, bf16[16,140,128]{2,1,0:T(8,128)(2,1)S(1)} %reshape_reshape.7, bf16[16,144,128]{2,1,0:T(8,128)(2,1)S(1)} %reshape_reshape.6), kind=kLoop, calls=%fused_computation.6 | loop fusion | flops 3538944 | bytes 2359296 | tf_op jit(solution)/shard_map/concatenate | solution.py:156
  7.3 6.6 %all-to-all-start = ((bf16[16,288,128]{2,1,0:T(8,128)(2,1)}), bf16[16,288,128]{2,1,0:T(8,128)(2,1)S(1)}, u32[]{:S(2)}, u32[]{:S(2)}) async-start(bf16[16,288,128]{2,1,0:T(8,128)(2,1)} %pad_maximum_fusion), calls=%async_computation | async-start | bytes 2359296 | tf_op jit(solution)/shard_map/all_to_all | solution.py:164
  13.8 0.0 copy-done.1
  13.8 0.7 %copy.16.lim_ref = s32[128,1]{1,0:T(8,128)} copy(s32[128,1]{0,1:T(1,128)S(1)} %multiply_bitcast_fusion) | data formatting | bytes 1024 | tf_op jit(solution)/shard_map/reshape | solution.py:175
  14.6 0.5 convolution_convert_fusion
  15.1 26.5 %all-to-all-done = bf16[16,288,128]{2,1,0:T(8,128)(2,1)S(1)} async-done(((bf16[16,288,128]{2,1,0:T(8,128)(2,1)}), bf16[16,288,128]{2,1,0:T(8,128)(2,1)S(1)}, u32[]{:S(2)}, u32[]{:S(2)}) %all-to-all-start) | async-done | bytes 1179680 | tf_op jit(solution)/shard_map/all_to_all | solution.py:164
  41.6 0.1 slice.37
  41.7 0.1 eq.140
  41.8 0.1 eq.136
  41.9 0.6 %reshape.81 = bf16[80,3584]{1,0:T(8,128)(2,1)S(1)} reshape(bf16[16,140,128]{2,1,0:T(8,128)(2,1)S(1)} %slice.38) | data formatting | bytes 1146880 | tf_op jit(solution)/shard_map/reshape | solution.py:166
  42.6 0.3 reshape.82
  42.8 1.2 %convolution_convert_fusion.3.pan_ref = bf16[128,2048]{1,0:T(8,128)(2,1)} fusion(bf16[144,2048]{1,0:T(8,128)(2,1)S(1)} %reshape.82, f32[144]{0:T(256)S(1)} %eq.140), kind=kOutput, calls=%fused_computation.5 | convolution fusion | flops 75778048 | bytes 1114688 | tf_op jit(solution)/shard_map/dot_general | solution.py:37
  44.1 1.4 %fusion.own_ref = bf16[128,3584]{1,0:T(8,128)(2,1)} fusion(bf16[80,3584]{1,0:T(8,128)(2,1)S(1)} %reshape.81, bf16[128,3584]{1,0:T(8,128)(2,1)S(1)} %convolution_convert_fusion, f32[80]{0:T(128)S(1)} %eq.136), kind=kOutput, calls=%fused_computation.1 | convolution fusion | flops 74786816 | bytes 2408768 | tf_op jit(solution)/shard_map/dot_general | solution.py:37
  45.5 14.3 %shard_map.95 = (bf16[128,8,1024]{2,1,0:T(8,128)(2,1)}, bf16[7,128,512]{2,1,0:T(8,128)(2,1)}) custom-call(bf16[128,3584]{1,0:T(8,128)(2,1)} %fusion.own_ref, bf16[128,2048]{1,0:T(8,128)(2,1)} %convolution_convert_fusion.3.pan_ref, f32[4,512]{1,0:T(4,128)} %uw_ref.1, bf16[7,512,1024]{2,1,0:T(8,128)(2,1)} %w_ref.1, f32[1,1024]{1,0:T(1,128)} %bitcast.38, ...), custom_call_target="tpu_custom_call" | custom-call | tf_op jit(solution)/shard_map/pallas_call | solution.py:93
  (11 shorter events, 0.2 us)
Async XLA Ops:
  0.6 3.6 %copy-start = (bf16[128,7,512]{2,0,1:T(8,128)(2,1)S(1)}, bf16[128,7,512]{2,0,1:T(8,128)(2,1)}, u32[]{:S(2)}) copy-start(bf16[128,7,512]{2,0,1:T(8,128)(2,1)} %param.9) | copy-start | bytes 2752516
  6.2 7.7 %copy-start.1 = (s32[128]{0:T(128)S(1)}, s32[128]{0:T(128)}, u32[]{:S(2)}) copy-start(s32[128]{0:T(128)} %param.12) | copy-start | bytes 1540
  7.3 34.3 %all-to-all-start = ((bf16[16,288,128]{2,1,0:T(8,128)(2,1)}), bf16[16,288,128]{2,1,0:T(8,128)(2,1)S(1)}, u32[]{:S(2)}, u32[]{:S(2)}) async-start(bf16[16,288,128]{2,1,0:T(8,128)(2,1)} %pad_maximum_fusion), calls=%async_computation | async-start | bytes 2359296 | tf_op jit(solution)/shard_map/all_to_all | solution.py:164

commit v10 on v9

--- a/solution.py
+++ b/solution.py
@@ -37,7 +37,7 @@
     return jnp.dot(picker.T, received, preferred_element_type=jnp.float32)
 
 
-def conv_kernel(own_ref, pan_ref, uw_ref, w_ref, b_ref, lim_ref, o_ref, nc_ref, ext_ref):
+def conv_kernel(own_ref, pan_ref, uw_ref, w_ref, b_ref, lim_ref, o_ref, nc_ref, ext_ref, out_ref):
     taps = w_ref.shape[0]
     streams, steps, block = o_ref.shape
     rows, _, channels = ext_ref.shape
@@ -80,7 +80,8 @@
     act = jnp.where(acc > 0, acc, jnp.exp(acc) - 1.0)
     act = act.reshape(steps, streams, block)
     for step in range(steps):
-        o_ref[:, step, :] = jnp.where(step < lim, act[step], 0.0).astype(o_ref.dtype)
+        out_ref[:, step, :] = jnp.where(step < lim, act[step], 0.0)
+    o_ref[...] = out_ref[...].astype(o_ref.dtype)
 
 
 def conv_call(owned, panels, up_weight, conv_weight, conv_bias, limit, steps):
@@ -109,7 +110,10 @@
             pl.BlockSpec((streams, steps, block), lambda n: (0, 0, n)),
             pl.BlockSpec((cache_width // channels, streams, channels), lambda n: (0, 0, 0)),
         ),
-        scratch_shapes=[pltpu.VMEM((rows, streams, channels), jnp.bfloat16)],
+        scratch_shapes=[
+            pltpu.VMEM((rows, streams, channels), jnp.bfloat16),
+            pltpu.VMEM((streams, steps, block), jnp.float32),
+        ],
         compiler_params=pltpu.CompilerParams(dimension_semantics=("arbitrary",)),
     )(owned, panels, up_weight, conv_weight, conv_bias.reshape(1, outward), limit)
 

time: 60 us -> 59 us (0.983)
  Pallas kernels: 14.3 us -> 13.2 us
    pallas_call x1, Pallas kernels: 14.3 us -> 13.2 us  [conv_call(): pl.pallas_call(conv_kernel, out_shape=(jax.ShapeDtypeStruct((streams, ste...]
where the time goes in v10:
time: 59 us; the launch traced here: 58.7 us
  waiting for transfers between devices  26.5 us (45%)
  Pallas kernels  13.2 us (22%)
  starting transfers between devices  6.56 us (11%)
  local copies, waits for them, and re-layouts  4.93 us (8%)
  matrix products  4.12 us (7%)
  other arithmetic  2.6 us (4%)
  between operations  0.83 us (1%)
    all_to_all x1, waiting for transfers between devices, body(): lax.all_to_all(joint, 'dec', split_axis=0, concat_axis=0, tiled=True)  26.5 us
    pallas_call x1, Pallas kernels, conv_call(): pl.pallas_call(conv_kernel, out_shape=(jax.ShapeDtypeStruct((streams, ste...  13.2 us
    all_to_all x1, starting transfers between devices, body(): lax.all_to_all(joint, 'dec', split_axis=0, concat_axis=0, tiled=True)  6.56 us
    dot_general x2, matrix products, settle(): return jnp.dot(picker.T, received, preferred_element_type=jnp.float32)  2.65 us
    unnamed x6, local copies, waits for them, and re-layouts  1.77 us
  transfers between devices with their start and end apart: 1, of which 1 were waited for; matrix products, arithmetic and copies ran while one was open for 2% of the time, Pallas kernels for 0%

profile of v10, /device:TPU:13, one launch (start us, length us, event | category | flops | bytes accessed | tf_op | source)
XLA Modules:
  0.0 58.7 jit_solution(4635791757519375362)
XLA Ops:
  0.6 0.0 copy-start
  0.6 0.8 %negate_select_fusion.1 = (s32[3,128]{1,0:T(4,128)S(1)}, s32[3,128]{1,0:T(4,128)S(1)}) fusion(s32[1,128]{1,0:T(1,128)} %bitcast.41, s32[1,128]{1,0:T(1,128)} %bitcast.39, s32[1,128]{1,0:T(1,128)} %bitcast.40), kind=kLoop, calls=%fused_computation.38 | loop fusion | flops 4224 | bytes 4608 | tf_op jit(solution)/shard_map/div | solution.py:135
  1.4 0.2 convert_reduce_fusion.1
  1.6 0.2 convert_reduce_fusion
  1.8 0.1 multiply_reduce_fusion.1
  1.9 0.1 multiply_reduce_fusion
  2.1 0.1 sub.13
  2.2 0.1 sub.15
  2.3 0.1 fusion.18
  2.4 1.1 %copy.17 = bf16[16,8,4,512]{3,1,2,0:T(8,128)(2,1)S(1)} copy(bf16[16,8,4,512]{3,2,1,0:T(4,128)(2,1)} %bitcast.35) | data formatting | bytes 1048576
  3.5 0.4 convolution_convert_fusion.2
  4.0 0.3 reshape_reshape.6
  4.2 0.0 copy-done
  4.2 0.6 %copy.15 = bf16[128,7,512]{0,2,1:T(8,128)(2,1)S(1)} copy(bf16[128,7,512]{2,0,1:T(8,128)(2,1)S(1)} %copy-done) | data formatting | bytes 1835008 | tf_op args[1]
  4.9 0.5 convolution_convert_fusion.1
  5.4 0.7 %reshape_reshape.7 = bf16[16,140,128]{2,1,0:T(8,128)(2,1)S(1)} reshape(bf16[80,3584]{1,0:T(8,128)(2,1)S(1)} %convolution_convert_fusion.1) | data formatting | bytes 1146880 | tf_op jit(solution)/shard_map/reshape;reshape | solution.py:163
  6.2 0.0 copy-start.1
  6.2 1.1 %pad_maximum_fusion = bf16[16,288,128]{2,1,0:T(8,128)(2,1)} fusion(bf16[16,4,128]{2,1,0:T(4,128)(2,1)S(1)} %reshape.80, bf16[16,140,128]{2,1,0:T(8,128)(2,1)S(1)} %reshape_reshape.7, bf16[16,144,128]{2,1,0:T(8,128)(2,1)S(1)} %reshape_reshape.6), kind=kLoop, calls=%fused_computation.6 | loop fusion | flops 3538944 | bytes 2359296 | tf_op jit(solution)/shard_map/concatenate | solution.py:160
  7.3 6.6 %all-to-all-start = ((bf16[16,288,128]{2,1,0:T(8,128)(2,1)}), bf16[16,288,128]{2,1,0:T(8,128)(2,1)S(1)}, u32[]{:S(2)}, u32[]{:S(2)}) async-start(bf16[16,288,128]{2,1,0:T(8,128)(2,1)} %pad_maximum_fusion), calls=%async_computation | async-start | bytes 2359296 | tf_op jit(solution)/shard_map/all_to_all | solution.py:168
  13.8 0.0 copy-done.1
  13.8 0.7 %copy.16.lim_ref = s32[128,1]{1,0:T(8,128)} copy(s32[128,1]{0,1:T(1,128)S(1)} %multiply_bitcast_fusion) | data formatting | bytes 1024 | tf_op jit(solution)/shard_map/reshape | solution.py:179
  14.6 0.5 convolution_convert_fusion
  15.1 26.5 %all-to-all-done = bf16[16,288,128]{2,1,0:T(8,128)(2,1)S(1)} async-done(((bf16[16,288,128]{2,1,0:T(8,128)(2,1)}), bf16[16,288,128]{2,1,0:T(8,128)(2,1)S(1)}, u32[]{:S(2)}, u32[]{:S(2)}) %all-to-all-start) | async-done | bytes 1179680 | tf_op jit(solution)/shard_map/all_to_all | solution.py:168
  41.6 0.1 slice.37
  41.7 0.1 eq.140
  41.8 0.1 eq.136
  41.9 0.6 %reshape.81 = bf16[80,3584]{1,0:T(8,128)(2,1)S(1)} reshape(bf16[16,140,128]{2,1,0:T(8,128)(2,1)S(1)} %slice.38) | data formatting | bytes 1146880 | tf_op jit(solution)/shard_map/reshape | solution.py:170
  42.6 0.3 reshape.82
  42.8 1.2 %convolution_convert_fusion.3.pan_ref = bf16[128,2048]{1,0:T(8,128)(2,1)} fusion(bf16[144,2048]{1,0:T(8,128)(2,1)S(1)} %reshape.82, f32[144]{0:T(256)S(1)} %eq.140), kind=kOutput, calls=%fused_computation.5 | convolution fusion | flops 75778048 | bytes 1114688 | tf_op jit(solution)/shard_map/dot_general | solution.py:37
  44.1 1.4 %fusion.own_ref = bf16[128,3584]{1,0:T(8,128)(2,1)} fusion(bf16[80,3584]{1,0:T(8,128)(2,1)S(1)} %reshape.81, bf16[128,3584]{1,0:T(8,128)(2,1)S(1)} %convolution_convert_fusion, f32[80]{0:T(128)S(1)} %eq.136), kind=kOutput, calls=%fused_computation.1 | convolution fusion | flops 74786816 | bytes 2408768 | tf_op jit(solution)/shard_map/dot_general | solution.py:37
  45.5 13.2 %shard_map.95 = (bf16[128,8,1024]{2,1,0:T(8,128)(2,1)}, bf16[7,128,512]{2,1,0:T(8,128)(2,1)}) custom-call(bf16[128,3584]{1,0:T(8,128)(2,1)} %fusion.own_ref, bf16[128,2048]{1,0:T(8,128)(2,1)} %convolution_convert_fusion.3.pan_ref, f32[4,512]{1,0:T(4,128)} %uw_ref.1, bf16[7,512,1024]{2,1,0:T(8,128)(2,1)} %w_ref.1, f32[1,1024]{1,0:T(1,128)} %bitcast.38, ...), custom_call_target="tpu_custom_call" | custom-call | tf_op jit(solution)/shard_map/pallas_call | solution.py:94
  (11 shorter events, 0.2 us)
Async XLA Ops:
  0.6 3.6 %copy-start = (bf16[128,7,512]{2,0,1:T(8,128)(2,1)S(1)}, bf16[128,7,512]{2,0,1:T(8,128)(2,1)}, u32[]{:S(2)}) copy-start(bf16[128,7,512]{2,0,1:T(8,128)(2,1)} %param.9) | copy-start | bytes 2752516
  6.2 7.7 %copy-start.1 = (s32[128]{0:T(128)S(1)}, s32[128]{0:T(128)}, u32[]{:S(2)}) copy-start(s32[128]{0:T(128)} %param.12) | copy-start | bytes 1540
  7.3 34.3 %all-to-all-start = ((bf16[16,288,128]{2,1,0:T(8,128)(2,1)}), bf16[16,288,128]{2,1,0:T(8,128)(2,1)S(1)}, u32[]{:S(2)}, u32[]{:S(2)}) async-start(bf16[16,288,128]{2,1,0:T(8,128)(2,1)} %pad_maximum_fusion), calls=%async_computation | async-start | bytes 2359296 | tf_op jit(solution)/shard_map/all_to_all | solution.py:168
